TPU v7x, 32 devices: a whole 2x2x4 slice. The times are simulated.
32 devices in a mesh: section: 2 (over core), fsdp: 2 (over y), expert: 8 (over z, x).
Axes of the slice: x: 2, y: 2, z: 4, core: 2. Of those that a mesh axis runs over, the one named last changes fastest.
Arguments:
- tokens: bfloat16 [2048, 2048], P(('fsdp', 'expert')), may hold values from -40 to 40
- norm_gain: float32 [2, 2048], P('section'), may hold values from 0.5 to 1.5
- router: bfloat16 [2, 2048, 32], P('section'), may hold values from -0.3125 to 0.3125
- w_gate: bfloat16 [2, 32, 2048, 768], P('section', 'expert', 'fsdp'), may hold values from -0.125 to 0.125
- w_up: bfloat16 [2, 32, 2048, 768], P('section', 'expert', 'fsdp'), may hold values from -0.125 to 0.125
- w_down: bfloat16 [2, 32, 768, 2048], P('section', 'expert', None, 'fsdp'), may hold values from -0.21875 to 0.21875
- routes: int32 [2, 2048, 6], P('section', ('fsdp', 'expert')), may hold values from 0 to 31, all different within a row; in each aligned block of 64 rows (0 to 63, 64 to 127, ..., all dimensions but the last counted through in order) at most 14 rows name the same one
Outputs:
- final_out: bfloat16 [2048, 2048], P(('fsdp', 'expert'), 'section')
- layer_stats: float32 [2], P('section')
Inputs may be any that keep to these rules, and one draw needn't show every extreme that they name: `routes`: each row names 6 different experts; in every aligned block of 64 rows of one layer no expert is named by more than 14 rows, a bound that some block reaches.
All inputs are finite; a program needn't handle non-finite values.
Results may differ from a plain program's by a relative error of at most 0.0065.
Values may be sent and summed in bfloat16 or wider, within the bound.
No kernel may reach another device: no remote copies, remote signals or barrier semaphores. Data moves between devices by JAX's collectives and lax.ppermute only.
A program may use at most 192 MiB of HBM per device.

v0:
```python
import jax
import jax.numpy as jnp
from jax import lax
from jax.sharding import PartitionSpec as P

TOP = 6
MB = 2


epsilon = 1e-06


def from_behind(value, axis, steps):
    count = lax.axis_size(axis)
    initial, last = (max(0, -steps), min(count, count - steps))
    return lax.ppermute(value, axis, [(source, source + steps) for source in range(initial, last)])


def rms_scaled(hidden_rows, gain_row):
    values = hidden_rows.astype(jnp.float32)
    scale = lax.rsqrt(jnp.mean(values * values, axis=-1, keepdims=True) + epsilon)
    return (values * scale * gain_row).astype(jnp.bfloat16)


def gate_weights(normed, router_weight, route_rows):
    logits = jnp.dot(normed, router_weight, preferred_element_type=jnp.float32)
    scores = jax.nn.sigmoid(logits)
    expert_ids = jnp.arange(router_weight.shape[1], dtype=jnp.int32)
    chosen_mask = (route_rows[:, :, None] == expert_ids[None, None, :]).astype(jnp.float32)
    chosen = jnp.sum(scores[:, None, :] * chosen_mask, axis=2)
    return chosen / jnp.sum(chosen, axis=1, keepdims=True)


def slot_positions(route_rows, experts_count, capacity):
    flat_routes = route_rows.reshape(-1)
    onehot = (flat_routes[:, None] == jnp.arange(experts_count, dtype=jnp.int32)[None, :]).astype(
        jnp.int32
    )
    before = jnp.cumsum(onehot, axis=0) - onehot
    slot_index = jnp.sum(before * onehot, axis=1)
    return (flat_routes * capacity + slot_index).reshape(route_rows.shape)


def expert_layer(entering, route_rows, gain_row, router_weight, weights, capacity, expert_devices):
    full_gate, full_up, full_down = weights
    width = entering.shape[1]
    experts_count = router_weight.shape[1]
    local_experts = full_gate.shape[1]
    normed = rms_scaled(entering, gain_row)
    mix_weights = gate_weights(normed, router_weight, route_rows)
    positions = slot_positions(route_rows, experts_count, capacity)
    slot_ids = jnp.arange(experts_count * capacity, dtype=jnp.int32)
    placing = jnp.any(positions[None, :, :] == slot_ids[:, None, None], axis=2).astype(jnp.bfloat16)
    buffer = jnp.dot(placing, normed, preferred_element_type=jnp.float32).astype(jnp.bfloat16)
    outgoing = buffer.reshape(expert_devices, local_experts * capacity, width)
    arrived = lax.all_to_all(outgoing, "expert", split_axis=0, concat_axis=0, tiled=True)
    arrived = arrived.reshape(expert_devices, local_experts, capacity, width)
    gate_part = jnp.einsum(
        "sjcd,jdh->sjch", arrived, full_gate[0], preferred_element_type=jnp.float32
    )
    up_part = jnp.einsum("sjcd,jdh->sjch", arrived, full_up[0], preferred_element_type=jnp.float32)
    inner_act = (jax.nn.silu(gate_part) * up_part).astype(jnp.bfloat16)
    produced = jnp.einsum(
        "sjch,jhd->sjcd", inner_act, full_down[0], preferred_element_type=jnp.float32
    ).astype(jnp.bfloat16)
    returned = lax.all_to_all(
        produced.reshape(expert_devices, local_experts * capacity, width),
        "expert",
        split_axis=0,
        concat_axis=0,
        tiled=True,
    )
    flat_out = returned.reshape(experts_count * capacity, width)
    picked = jnp.take(flat_out, positions, axis=0)
    branch_sum = jnp.sum(mix_weights[:, :, None] * picked.astype(jnp.float32), axis=1)
    return (entering.astype(jnp.float32) + branch_sum).astype(jnp.bfloat16)


def body(tokens, norm_gain, router, w_gate, w_up, w_down, routes):
    section_index = lax.axis_index("section")
    expert_devices = lax.axis_size("expert")
    token_rows = tokens.shape[0]
    width = tokens.shape[1]
    micro_rows = token_rows // MB
    experts_count = router.shape[2]
    capacity = (7 * micro_rows * TOP + 6 * experts_count - 1) // (6 * experts_count)
    gain_row = norm_gain[0]
    router_weight = router[0]
    route_all = routes[0]
    carried = jnp.zeros((micro_rows, width), jnp.bfloat16)
    stat_total = jnp.zeros((), jnp.float32)
    finished_parts = []
    for period in range(MB + 1):
        tick_gate, tick_up = (
            lax.all_gather(w_gate, "fsdp", axis=2, tiled=True),
            lax.all_gather(w_up, "fsdp", axis=2, tiled=True),
        )
        tick_down = lax.all_gather(w_down, "fsdp", axis=3, tiled=True)
        current = (tick_gate, tick_up, tick_down)
        if period < MB:
            arriving = tokens[period * micro_rows : (period + 1) * micro_rows]
        else:
            arriving = jnp.zeros((micro_rows, width), jnp.bfloat16)
        entering = jnp.where(section_index == 0, arriving, carried)
        micro_index = jnp.clip(period - section_index, 0, MB - 1)
        route_rows = lax.dynamic_slice_in_dim(route_all, micro_index * micro_rows, micro_rows, 0)
        leaving = expert_layer(
            entering, route_rows, gain_row, router_weight, current, capacity, expert_devices
        )
        counted = ((period - section_index >= 0) & (period - section_index < MB)).astype(
            jnp.float32
        )
        values = leaving.astype(jnp.float32)
        square_sum = counted * jnp.sum(values * values)
        stat_total = stat_total + lax.psum(square_sum, ("fsdp", "expert"))
        if period < MB:
            carried = from_behind(leaving, "section", 1)
        if period >= 1:
            finished_parts.append(leaving)
    token_total = token_rows * lax.axis_size("fsdp") * expert_devices
    layer_stats = jnp.sqrt(stat_total / (token_total * width)).reshape(1)
    finished = jnp.concatenate(finished_parts, axis=0)
    half_width = width // 2
    front_half = from_behind(finished[:, :half_width], "section", -1)
    final_out = jnp.where(section_index == 0, front_half, finished[:, half_width:])
    return (final_out, layer_stats)


def solution(mesh):
    in_specs = (
        P(("fsdp", "expert"), None),
        P("section", None),
        P("section", None, None),
        P("section", "expert", "fsdp", None),
        P("section", "expert", "fsdp", None),
        P("section", "expert", None, "fsdp"),
        P("section", ("fsdp", "expert"), None),
    )
    out_specs = (P(("fsdp", "expert"), "section"), P("section"))
    return jax.shard_map(body, mesh=mesh, in_specs=in_specs, out_specs=out_specs, check_vma=False)
```

profile of v0, /device:TPU:0, one launch (start us, length us, event | category | flops | bytes accessed | tf_op | source)
XLA Modules:
  0.0 869.0 jit_solution(7443549823910460913)
XLA Ops:
  12.5 49.7 %all_to_all.30 = bf16[8,56,2048]{2,1,0:T(8,128)(2,1)S(1)} all-to-all(bf16[8,56,2048]{2,1,0:T(8,128)(2,1)S(1)} %bitcast.238), channel_id=1, replica_groups=mesh['section'=2,'fsdp'=2,'expert'=8] {'expert'}, dimensions={0} | all-to-all | bytes 3670016 | tf_op jit(solution)/shard_map/all_to_all | solution.py:56
  63.2 100.6 %all-gather.6.cloned.1.call-done = bf16[1,4,2048,768]{3,2,1,0:T(8,128)(2,1)} async-done(((bf16[1,4,1024,768]{3,2,1,0:T(8,128)(2,1)}), bf16[1,4,2048,768]{3,2,1,0:T(8,128)(2,1)}) %all-gather.6.cloned.1.call-update) | async-done | bytes 12582928 | tf_op jit(solution)/shard_map/all_gather | solution.py:96
  163.8 8.2 fusion.10
  172.0 145.9 %all-gather.8.cloned.1.call-done = bf16[1,4,768,2048]{3,2,1,0:T(8,128)(2,1)} async-done(((bf16[1,4,768,1024]{3,2,1,0:T(8,128)(2,1)}), bf16[1,4,768,2048]{3,2,1,0:T(8,128)(2,1)}) %all-gather.8.cloned.1.call-update) | async-done | bytes 12582928 | tf_op jit(solution)/shard_map/all_gather | solution.py:98
  317.9 153.1 %all-gather.4.cloned.1.call-done = bf16[1,4,2048,768]{3,2,1,0:T(8,128)(2,1)} async-done(((bf16[1,4,1024,768]{3,2,1,0:T(8,128)(2,1)}), bf16[1,4,2048,768]{3,2,1,0:T(8,128)(2,1)}) %all-gather.4.cloned.1.call-update) | async-done | bytes 12582928 | tf_op jit(solution)/shard_map/all_gather | solution.py:95
  471.0 14.3 %fusion.33 = bf16[8,4,14,2048]{3,2,0,1:T(8,128)(2,1)} fusion(bf16[1,4,768,2048]{3,2,1,0:T(8,128)(2,1)} %all-gather.8.cloned.1.call-done, f32[4,8,14,768]{3,2,1,0:T(8,128)} %fusion.10, bf16[1,4,2048,768]{3,2,1,0:T(8,128)(2,1)} %all-gather.4.cloned.1.call-done, bf16[8,4,14,2048]{3,0,2,1:T(8,128)(2,1)S(1)} %bitcast.232), kind=kOutput, calls=%fused_computation.32 | convolution fusion | flops 2821554176 | bytes 30212096 | tf_op jit(solution)/shard_map/sjch,jhd->sjcd/dot_general | solution.py:63
  485.3 2.6 copy.131
  490.1 5.5 all-to-all-start.1
  500.3 37.7 %all-to-all-done.1 = bf16[8,56,2048]{2,1,0:T(8,128)(2,1)S(1)} async-done(((bf16[8,56,2048]{2,1,0:T(8,128)(2,1)}), bf16[8,56,2048]{2,1,0:T(8,128)(2,1)S(1)}, u32[]{:S(2)}, u32[]{:S(2)}) %all-to-all-start.1) | async-done | bytes 1835040 | tf_op jit(solution)/shard_map/all_to_all | solution.py:66
  542.2 4.3 multiply_reduce_fusion.2
  550.6 47.2 %all_to_all.31 = bf16[8,56,2048]{2,1,0:T(8,128)(2,1)S(1)} all-to-all(bf16[8,56,2048]{2,1,0:T(8,128)(2,1)S(1)} %bitcast.237), channel_id=1, replica_groups=mesh['section'=2,'fsdp'=2,'expert'=8] {'expert'}, dimensions={0} | all-to-all | bytes 3670016 | tf_op jit(solution)/shard_map/all_to_all | solution.py:56
  598.7 8.2 fusion.8
  606.9 14.3 %fusion.30 = bf16[8,4,14,2048]{3,2,0,1:T(8,128)(2,1)} fusion(bf16[1,4,768,2048]{3,2,1,0:T(8,128)(2,1)} %all-gather.8.cloned.1.call-done, f32[4,8,14,768]{3,2,1,0:T(8,128)} %fusion.8, bf16[1,4,2048,768]{3,2,1,0:T(8,128)(2,1)} %all-gather.4.cloned.1.call-done, bf16[8,4,14,2048]{3,0,2,1:T(8,128)(2,1)S(1)} %bitcast.236), kind=kOutput, calls=%fused_computation.31 | convolution fusion | flops 2821554176 | bytes 30212096 | tf_op jit(solution)/shard_map/sjch,jhd->sjcd/dot_general | solution.py:63
  621.2 2.6 copy.145
  626.1 4.0 all-to-all-start.3
  635.5 37.2 %all-to-all-done.3 = bf16[8,56,2048]{2,1,0:T(8,128)(2,1)S(1)} async-done(((bf16[8,56,2048]{2,1,0:T(8,128)(2,1)}), bf16[8,56,2048]{2,1,0:T(8,128)(2,1)S(1)}, u32[]{:S(2)}, u32[]{:S(2)}) %all-to-all-start.3) | async-done | bytes 1835040 | tf_op jit(solution)/shard_map/all_to_all | solution.py:66
  676.8 4.3 multiply_reduce_fusion.1
  685.1 47.4 %all_to_all.32 = bf16[8,56,2048]{2,1,0:T(8,128)(2,1)S(1)} all-to-all(bf16[8,56,2048]{2,1,0:T(8,128)(2,1)S(1)} %bitcast.241), channel_id=1, replica_groups=mesh['section'=2,'fsdp'=2,'expert'=8] {'expert'}, dimensions={0} | all-to-all | bytes 3670016 | tf_op jit(solution)/shard_map/all_to_all | solution.py:56
  733.5 8.2 fusion.6
  741.7 14.4 %fusion.27 = bf16[8,4,14,2048]{3,2,0,1:T(8,128)(2,1)} fusion(bf16[1,4,768,2048]{3,2,1,0:T(8,128)(2,1)} %all-gather.8.cloned.1.call-done, f32[4,8,14,768]{3,2,1,0:T(8,128)} %fusion.6, bf16[1,4,2048,768]{3,2,1,0:T(8,128)(2,1)} %all-gather.4.cloned.1.call-done, bf16[8,4,14,2048]{3,0,2,1:T(8,128)(2,1)S(1)} %bitcast.234), kind=kOutput, calls=%fused_computation.30 | convolution fusion | flops 2821554176 | bytes 30212096 | tf_op jit(solution)/shard_map/sjch,jhd->sjcd/dot_general | solution.py:63
  760.9 4.1 all-to-all-start.5
  767.0 40.7 %all-to-all-done.5 = bf16[8,56,2048]{2,1,0:T(8,128)(2,1)S(1)} async-done(((bf16[8,56,2048]{2,1,0:T(8,128)(2,1)}), bf16[8,56,2048]{2,1,0:T(8,128)(2,1)S(1)}, u32[]{:S(2)}, u32[]{:S(2)}) %all-to-all-start.5) | async-done | bytes 1835040 | tf_op jit(solution)/shard_map/all_to_all | solution.py:66
  811.8 4.3 multiply_reduce_fusion
  820.1 39.4 %psum.25 = f32[]{:T(128)} all-reduce(f32[]{:T(128)S(6)} %add.122), channel_id=1, replica_groups=mesh['section'=2,'fsdp'=2,'expert'=8] {'fsdp','expert'}, use_global_device_ids=true, to_apply=%region_25.27 | all-reduce | flops 1 | bytes 8 | tf_op jit(solution)/shard_map/psum | solution.py:115
  (158 shorter events, 52.8 us)
Async XLA Ops:
  7.2 491.4 %copy-start = (bf16[1,2048,32]{1,2,0:T(8,128)(2,1)S(1)}, bf16[1,2048,32]{1,2,0:T(8,128)(2,1)}, u32[]{:S(2)}) copy-start(bf16[1,2048,32]{1,2,0:T(8,128)(2,1)} %param.11) | copy-start | bytes 393220
  7.2 156.6 %all-gather.6.cloned.1.call-start = ((), (), s32[]{:S(2)}) async-start(), calls=%async_computation.7 | async-start | bytes 18874368 | tf_op jit(solution)/shard_map/all_gather | solution.py:96
  7.9 310.0 %all-gather.8.cloned.1.call-start = ((), (), s32[]{:S(2)}) async-start(), calls=%async_computation.8 | async-start | bytes 18874368 | tf_op jit(solution)/shard_map/all_gather | solution.py:98
  8.7 462.3 %all-gather.4.cloned.1.call-start = ((), (), s32[]{:S(2)}) async-start(), calls=%async_computation.6 | async-start | bytes 18874368 | tf_op jit(solution)/shard_map/all_gather | solution.py:95
  9.6 486.1 %copy-start.13 = (s32[1,64,6]{1,0,2:T(1,128)}, s32[1,64,6]{1,0,2:T(1,128)S(1)}, u32[]{:S(2)}) copy-start(s32[1,64,6]{1,0,2:T(1,128)S(1)} %get-tuple-element.26) | copy-start | bytes 4612
  490.1 48.0 %all-to-all-start.1 = ((bf16[8,56,2048]{2,1,0:T(8,128)(2,1)}), bf16[8,56,2048]{2,1,0:T(8,128)(2,1)S(1)}, u32[]{:S(2)}, u32[]{:S(2)}) async-start(bf16[8,56,2048]{2,1,0:T(8,128)(2,1)} %copy.132), calls=%async_computation.1 | async-start | bytes 3670016 | tf_op jit(solution)/shard_map/all_to_all | solution.py:66
  497.4 40.7 %copy-start.19 = (s32[384]{0:T(512)}, s32[384]{0:T(512)S(1)}, u32[]{:S(2)}) copy-start(s32[384]{0:T(512)S(1)} %fusion.117) | copy-start | bytes 4612
  542.2 4.3 copy-start.8
  542.2 6.3 copy-start.14
  542.2 6.3 copy-start.22
  547.2 2.4 collective-permute-start
  549.8 84.6 %copy-start.1 = (bf16[64,2048]{1,0:T(8,128)(2,1)}, bf16[64,2048]{1,0:T(8,128)(2,1)S(1)}, u32[]{:S(2)}) copy-start(bf16[64,2048]{1,0:T(8,128)(2,1)S(1)} %get-tuple-element.20) | copy-start | bytes 786436
  626.0 4.3 copy-start.20
  626.1 46.6 %all-to-all-start.3 = ((bf16[8,56,2048]{2,1,0:T(8,128)(2,1)}), bf16[8,56,2048]{2,1,0:T(8,128)(2,1)S(1)}, u32[]{:S(2)}, u32[]{:S(2)}) async-start(bf16[8,56,2048]{2,1,0:T(8,128)(2,1)} %copy.146), calls=%async_computation.3 | async-start | bytes 3670016 | tf_op jit(solution)/shard_map/all_to_all | solution.py:66
  676.8 4.3 copy-start.2
  676.8 6.3 copy-start.23
  681.8 2.4 collective-permute-start.1
  684.2 81.8 %copy-start.5 = (bf16[64,2048]{1,0:T(8,128)(2,1)}, bf16[64,2048]{1,0:T(8,128)(2,1)S(1)}, u32[]{:S(2)}) copy-start(bf16[64,2048]{1,0:T(8,128)(2,1)S(1)} %collective-permute-done.1) | copy-start | bytes 786436
  760.9 4.1 copy-start.21
  760.9 4.3 copy-start.24
  760.9 46.7 %all-to-all-start.5 = ((bf16[8,56,2048]{2,1,0:T(8,128)(2,1)}), bf16[8,56,2048]{2,1,0:T(8,128)(2,1)S(1)}, u32[]{:S(2)}, u32[]{:S(2)}) async-start(bf16[8,56,2048]{2,1,0:T(8,128)(2,1)} %copy.160), calls=%async_computation.5 | async-start | bytes 3670016 | tf_op jit(solution)/shard_map/all_to_all | solution.py:66
  811.8 4.3 copy-start.6
  811.8 5.1 copy-start.4
  816.9 43.3 %collective-permute-start.2 = (bf16[128,1024]{1,0:T(8,128)(2,1)S(1)}, bf16[128,1024]{1,0:T(8,128)(2,1)S(1)}, u32[]{:S(2)}, u32[]{:S(2)}) collective-permute-start(bf16[128,1024]{1,0:T(8,128)(2,1)S(1)} %fusion.105), channel_id=1, source_target_pairs={{16,0},{17,1},{18,2},{19,3},{20,4},{21,5},{22,6},{23,7},{24,8},{25... | collective-permute-start | bytes 786440 | tf_op jit(solution)/shard_map/ppermute | solution.py:16
  (10 other events, 19.1 us)
Sparse Core Ops, SparseCore 0:
  9.5 154.2 all-gather.5
  165.4 152.4 all-gather.7
  319.5 151.4 all-gather.3
where the time goes:
time: 883 us; the launch traced here: 869 us
  waiting for transfers between devices  519 us (59%)
  blocking collectives  184 us (21%)
  matrix products  70.5 us (8%)
  local copies, waits for them, and re-layouts  39 us (4%)
  other arithmetic  20.8 us (2%)
  between operations  18.3 us (2%)
  starting transfers between devices  17.5 us (2%)
    all_gather x1, waiting for transfers between devices, body(): lax.all_gather(w_gate, 'fsdp', axis=2, tiled=True)  153 us
    all_gather x1, waiting for transfers between devices, body(): tick_down = lax.all_gather(w_down, 'fsdp', axis=3, tiled=True)  146 us
    all_to_all x3, blocking collectives, expert_layer(): lax.all_to_all(outgoing, 'expert', split_axis=0, concat_axis=0, tiled=True)  144 us
    all_to_all x3, waiting for transfers between devices, expert_layer(): lax.all_to_all(produced.reshape(expert_devices, local_experts * capacity,...  116 us
    all_gather x1, waiting for transfers between devices, body(): lax.all_gather(w_up, 'fsdp', axis=2, tiled=True)  101 us
    dot_general x3, matrix products, expert_layer(): jnp.einsum('sjch,jhd->sjcd', inner_act, full_down[0], preferred_element_t...  43 us
    psum x1, blocking collectives, body(): stat_total = stat_total + lax.psum(square_sum, ('fsdp', 'expert'))  39.4 us
    dot_general x3, matrix products, expert_layer(): jnp.einsum('sjcd,jdh->sjch', arrived, full_up[0], preferred_element_type=...  24.5 us
  transfers between devices with their start and end apart: 9, of which 8 were waited for; matrix products, arithmetic and copies ran while one was open for 3% of the time, Pallas kernels for 0%

commit v1 on v0

v1 whole, which is shorter than its diff:
```python
import jax
import jax.numpy as jnp
from jax import lax
from jax.sharding import PartitionSpec as P

TOP = 6
BLOCK = 64


epsilon = 1e-06


def other_section(value):
    return lax.ppermute(value, "section", [(0, 1), (1, 0)])


def rms_scaled(hidden_rows, gain_row):
    values = hidden_rows.astype(jnp.float32)
    scale = lax.rsqrt(jnp.mean(values * values, axis=-1, keepdims=True) + epsilon)
    return (values * scale * gain_row).astype(jnp.bfloat16)


def gate_weights(normed, router_weight, route_rows):
    logits = jnp.dot(normed, router_weight, preferred_element_type=jnp.float32)
    scores = jax.nn.sigmoid(logits)
    expert_ids = jnp.arange(router_weight.shape[1], dtype=jnp.int32)
    chosen_mask = (route_rows[:, :, None] == expert_ids[None, None, :]).astype(jnp.float32)
    chosen = jnp.sum(scores[:, None, :] * chosen_mask, axis=2)
    return chosen / jnp.sum(chosen, axis=1, keepdims=True)


def slot_positions(route_rows, experts_count, capacity):
    flat_routes = route_rows.reshape(-1)
    onehot = (flat_routes[:, None] == jnp.arange(experts_count, dtype=jnp.int32)[None, :]).astype(
        jnp.int32
    )
    before = jnp.cumsum(onehot, axis=0) - onehot
    slot_index = jnp.sum(before * onehot, axis=1)
    return (flat_routes * capacity + slot_index).reshape(route_rows.shape)


def expert_layer(entering, route_rows, gain_row, router_weight, weights, capacity):
    gate_w, up_w, down_w = weights
    width = entering.shape[1]
    experts_count = router_weight.shape[1]
    local_experts, chunk, hidden_units = gate_w.shape
    fsdp_count = lax.axis_size("fsdp")
    expert_devices = lax.axis_size("expert")
    peers = fsdp_count * expert_devices
    normed = rms_scaled(entering, gain_row)
    mix_weights = gate_weights(normed, router_weight, route_rows)
    positions = slot_positions(route_rows, experts_count, capacity)
    slot_ids = jnp.arange(experts_count * capacity, dtype=jnp.int32)
    placing = jnp.any(positions[None, :, :] == slot_ids[:, None, None], axis=2).astype(jnp.bfloat16)
    buffer = jnp.dot(placing, normed, preferred_element_type=jnp.float32).astype(jnp.bfloat16)
    outgoing = (
        buffer.reshape(expert_devices, local_experts * capacity, fsdp_count, chunk)
        .transpose(2, 0, 1, 3)
        .reshape(peers, local_experts * capacity, chunk)
    )
    arrived = lax.all_to_all(outgoing, ("fsdp", "expert"), 0, 0, tiled=True)
    arrived = arrived.reshape(peers, local_experts, capacity, chunk)
    gate_part = jnp.einsum("sjcd,jdh->sjch", arrived, gate_w, preferred_element_type=jnp.float32)
    up_part = jnp.einsum("sjcd,jdh->sjch", arrived, up_w, preferred_element_type=jnp.float32)
    both = jnp.concatenate([gate_part, up_part], axis=-1)
    summed = lax.psum_scatter(both, "fsdp", scatter_dimension=0, tiled=True)
    gate_sum = summed[..., :hidden_units]
    up_sum = summed[..., hidden_units:]
    inner_act = (jax.nn.silu(gate_sum) * up_sum).astype(jnp.bfloat16)
    inner_all = lax.all_gather(inner_act, "fsdp", axis=0, tiled=True)
    produced = jnp.einsum(
        "sjch,jhd->sjcd", inner_all, down_w, preferred_element_type=jnp.float32
    ).astype(jnp.bfloat16)
    returned = lax.all_to_all(
        produced.reshape(peers, local_experts * capacity, chunk),
        ("fsdp", "expert"),
        0,
        0,
        tiled=True,
    )
    flat_out = (
        returned.reshape(fsdp_count, expert_devices, local_experts * capacity, chunk)
        .transpose(1, 2, 0, 3)
        .reshape(experts_count * capacity, width)
    )
    picked = jnp.take(flat_out, positions, axis=0)
    branch_sum = jnp.sum(mix_weights[:, :, None] * picked.astype(jnp.float32), axis=1)
    return (entering.astype(jnp.float32) + branch_sum).astype(jnp.bfloat16)


def body(tokens, norm_gain, router, w_gate, w_up, w_down, routes):
    section_index = lax.axis_index("section")
    sections = lax.axis_size("section")
    token_rows, width = tokens.shape
    piece = token_rows // sections
    experts_count = router.shape[2]
    block_capacity = (7 * BLOCK * TOP + 6 * experts_count - 1) // (6 * experts_count)
    capacity = block_capacity * (piece // BLOCK)
    own_weights = (w_gate[0], w_up[0], w_down[0])
    other_weights = tuple(other_section(w) for w in own_weights)
    own_small = (norm_gain[0], router[0], routes[0])
    other_small = tuple(other_section(v) for v in own_small)
    hidden = lax.dynamic_slice_in_dim(tokens, section_index * piece, piece, 0)
    squares = []
    for layer in range(sections):
        mine = section_index == layer
        gain_row, router_weight, route_all = [
            jnp.where(mine, a, b) for a, b in zip(own_small, other_small)
        ]
        weights = tuple(jnp.where(mine, a, b) for a, b in zip(own_weights, other_weights))
        route_rows = lax.dynamic_slice_in_dim(route_all, section_index * piece, piece, 0)
        hidden = expert_layer(hidden, route_rows, gain_row, router_weight, weights, capacity)
        values = hidden.astype(jnp.float32)
        squares.append(jnp.sum(values * values))
    totals = lax.psum(jnp.stack(squares), ("section", "fsdp", "expert"))
    token_total = token_rows * lax.axis_size("fsdp") * lax.axis_size("expert")
    stats = jnp.sqrt(totals / (token_total * width))
    layer_stats = lax.dynamic_slice_in_dim(stats, section_index, 1, 0)
    half_width = width // 2
    keep = lax.dynamic_slice_in_dim(hidden, section_index * half_width, half_width, 1)
    send = lax.dynamic_slice_in_dim(hidden, (1 - section_index) * half_width, half_width, 1)
    arrived = other_section(send)
    final_out = jnp.where(
        section_index == 0,
        jnp.concatenate([keep, arrived], axis=0),
        jnp.concatenate([arrived, keep], axis=0),
    )
    return (final_out, layer_stats)


def solution(mesh):
    in_specs = (
        P(("fsdp", "expert"), None),
        P("section", None),
        P("section", None, None),
        P("section", "expert", "fsdp", None),
        P("section", "expert", "fsdp", None),
        P("section", "expert", None, "fsdp"),
        P("section", ("fsdp", "expert"), None),
    )
    out_specs = (P(("fsdp", "expert"), "section"), P("section"))
    return jax.shard_map(body, mesh=mesh, in_specs=in_specs, out_specs=out_specs, check_vma=False)
```

time: 883 us -> 550 us (0.62)
  waiting for transfers between devices: 519 us -> 271 us
  blocking collectives: 184 us -> 141 us
  matrix products: 70.5 us -> 37.7 us
    all_gather x3 -> x2, waiting for transfers between devices: 400 us -> 50.3 us  [expert_layer(): inner_all = lax.all_gather(inner_act, 'fsdp', axis=0, tiled=True)]
    reduce_scatter x0 -> x2, waiting for transfers between devices: none -> 133 us  [expert_layer(): summed = lax.psum_scatter(both, 'fsdp', scatter_dimension=0, tiled=True)]
    all_to_all x3 -> x2, blocking collectives: 144 us -> 101 us  [expert_layer(): arrived = lax.all_to_all(outgoing, ('fsdp', 'expert'), 0, 0, tiled=True)]
    all_to_all x3 -> x2, waiting for transfers between devices: 116 us -> 79.2 us  [expert_layer(): lax.all_to_all(produced.reshape(peers, local_experts * capacity, chunk),...]
    dot_general x6, matrix products: 67.5 us -> 33.5 us  [the longest x2 11.6 us: expert_layer(): jnp.einsum('sjch,jhd->sjcd', inner_all, down_w, preferred_element_type=jn...]
    reshape x3 -> x8, local copies, waits for them, and re-layouts: 6.72 us -> 17.7 us  [the longest x4 9.41 us: expert_layer(): buffer.reshape(expert_devices, local_experts * capacity, fsdp_count, chunk)]
  transfers between devices with their start and end apart: 9 -> 13, of which waited for: 8 -> 8; matrix products, arithmetic and copies ran while one was open for 3% -> 5% of each run, Pallas kernels for 0% -> 0%
where the time goes in v1:
time: 550 us; the launch traced here: 543 us
  waiting for transfers between devices  271 us (49%)
  blocking collectives  141 us (26%)
  matrix products  37.7 us (7%)
  local copies, waits for them, and re-layouts  32.7 us (6%)
  other arithmetic  29.4 us (5%)
  starting transfers between devices  16.5 us (3%)
  between operations  14.7 us (3%)
    reduce_scatter x2, waiting for transfers between devices, expert_layer(): summed = lax.psum_scatter(both, 'fsdp', scatter_dimension=0, tiled=True)  133 us
    all_to_all x2, blocking collectives, expert_layer(): arrived = lax.all_to_all(outgoing, ('fsdp', 'expert'), 0, 0, tiled=True)  101 us
    all_to_all x2, waiting for transfers between devices, expert_layer(): lax.all_to_all(produced.reshape(peers, local_experts * capacity, chunk),...  79.2 us
    all_gather x2, waiting for transfers between devices, expert_layer(): inner_all = lax.all_gather(inner_act, 'fsdp', axis=0, tiled=True)  50.3 us
    psum x1, blocking collectives, body(): totals = lax.psum(jnp.stack(squares), ('section', 'fsdp', 'expert'))  39.4 us
    all_to_all x2, starting transfers between devices, expert_layer(): lax.all_to_all(produced.reshape(peers, local_experts * capacity, chunk),...  11.7 us
    dot_general x2, matrix products, expert_layer(): jnp.einsum('sjch,jhd->sjcd', inner_all, down_w, preferred_element_type=jn...  11.6 us
  transfers between devices with their start and end apart: 13, of which 8 were waited for; matrix products, arithmetic and copies ran while one was open for 5% of the time, Pallas kernels for 0%

profile of v1, /device:TPU:0, one launch (start us, length us, event | category | flops | bytes accessed | tf_op | source)
XLA Modules:
  0.0 542.8 jit_solution(15079160899732492798)
XLA Ops:
  10.1 7.8 %collective-permute-done = s32[128,6]{0,1:T(8,128)S(1)} collective-permute-done((s32[128,6]{0,1:T(8,128)S(1)}, s32[128,6]{0,1:T(8,128)S(1)}, u32[]{:S(2)}, u32[]{:S(2)}) %collective-permute-start) | collective-permute-done | bytes 3104 | tf_op jit(solution)/shard_map/ppermute | solution.py:14
  24.3 4.6 reshape.156
  29.5 52.1 %all_to_all.20 = bf16[16,56,1024]{2,1,0:T(8,128)(2,1)S(1)} all-to-all(bf16[16,56,1024]{2,1,0:T(8,128)(2,1)S(1)} %bitcast.172), channel_id=1, replica_groups=mesh['section'=2,'fsdp'=2,'expert'=8] {'fsdp','expert'}, dimensions={0} | all-to-all | bytes 3670016 | tf_op jit(solution)/shard_map/all_to_all | solution.py:61
  82.6 4.6 fusion.27
  87.1 4.6 fusion.30
  91.7 3.1 pad_maximum_fusion
  97.0 66.7 %reduce-scatter.3.cloned.1.call-done = f32[8,4,14,1536]{3,0,2,1:T(8,128)} async-done(((f32[16,4,14,1536]{3,0,2,1:T(8,128)}), f32[8,4,14,1536]{3,0,2,1:T(8,128)}) %reduce-scatter.3.cloned.1.call-update) | async-done | bytes 2752528 | tf_op jit(solution)/shard_map/reduce_scatter | solution.py:66
  163.7 3.0 fusion.43
  166.8 25.1 %all-gather.3.cloned.1.call-done = bf16[16,4,14,768]{3,0,2,1:T(8,128)(2,1)} async-done(((bf16[8,4,14,768]{3,0,2,1:T(8,128)(2,1)}), bf16[16,4,14,768]{3,0,2,1:T(8,128)(2,1)}) %all-gather.3.cloned.1.call-update) | async-done | bytes 1376272 | tf_op jit(solution)/shard_map/all_gather | solution.py:70
  191.9 4.9 fusion.24
  199.1 5.7 %all-to-all-start.1 = ((bf16[16,56,1024]{2,1,0:T(8,128)(2,1)}), bf16[16,56,1024]{2,1,0:T(8,128)(2,1)S(1)}, u32[]{:S(2)}, u32[]{:S(2)}) async-start(bf16[16,56,1024]{2,1,0:T(8,128)(2,1)} %copy.68), calls=%async_computation.2 | async-start | bytes 3670016 | tf_op jit(solution)/shard_map/all_to_all | solution.py:74
  209.0 39.2 %all-to-all-done.1 = bf16[16,56,1024]{2,1,0:T(8,128)(2,1)S(1)} async-done(((bf16[16,56,1024]{2,1,0:T(8,128)(2,1)}), bf16[16,56,1024]{2,1,0:T(8,128)(2,1)S(1)}, u32[]{:S(2)}, u32[]{:S(2)}) %all-to-all-start.1) | async-done | bytes 1835040 | tf_op jit(solution)/shard_map/all_to_all | solution.py:74
  254.7 4.2 multiply_reduce_fusion.1
  264.7 49.3 %all_to_all.21 = bf16[16,56,1024]{2,1,0:T(8,128)(2,1)S(1)} all-to-all(bf16[16,56,1024]{2,1,0:T(8,128)(2,1)S(1)} %bitcast.174), channel_id=1, replica_groups=mesh['section'=2,'fsdp'=2,'expert'=8] {'fsdp','expert'}, dimensions={0} | all-to-all | bytes 3670016 | tf_op jit(solution)/shard_map/all_to_all | solution.py:61
  315.1 6.4 %fusion.36 = f32[16,4,14,768]{3,0,2,1:T(8,128)S(1)} fusion(bf16[16,4,14,1024]{3,0,2,1:T(8,128)(2,1)S(1)} %bitcast.178, bf16[4,1024,768]{2,1,0:T(8,128)(2,1)} %collective-permute-done.4, pred[]{:T(512)S(6)} %eq.124, bf16[1,4,1024,768]{3,2,1,0:T(8,128)(2,1)} %param.12), kind=kOutput, calls=%fused_computation.36 | convolution fusion | flops 1412431872 | bytes 17170432 | tf_op jit(solution)/shard_map/sjcd,jdh->sjch/dot_general | solution.py:63
  321.5 6.4 %fusion.39 = f32[16,4,14,768]{3,0,2,1:T(8,128)S(1)} fusion(bf16[16,4,14,1024]{3,0,2,1:T(8,128)(2,1)S(1)} %bitcast.179, bf16[4,1024,768]{2,1,0:T(8,128)(2,1)} %collective-permute-done.5, pred[]{:T(512)S(6)} %eq.124, bf16[1,4,1024,768]{3,2,1,0:T(8,128)(2,1)} %param.13), kind=kOutput, calls=%fused_computation.37 | convolution fusion | flops 1412431872 | bytes 17170432 | tf_op jit(solution)/shard_map/sjcd,jdh->sjch/dot_general | solution.py:64
  327.8 3.1 pad_maximum_fusion.1
  331.1 66.3 %reduce-scatter.5.cloned.1.call-done = f32[8,4,14,1536]{3,0,2,1:T(8,128)} async-done(((f32[16,4,14,1536]{3,0,2,1:T(8,128)}), f32[8,4,14,1536]{3,0,2,1:T(8,128)}) %reduce-scatter.5.cloned.1.call-update) | async-done | bytes 2752528 | tf_op jit(solution)/shard_map/reduce_scatter | solution.py:66
  400.4 25.1 %all-gather.5.cloned.1.call-done = bf16[16,4,14,768]{3,0,2,1:T(8,128)(2,1)} async-done(((bf16[8,4,14,768]{3,0,2,1:T(8,128)(2,1)}), bf16[16,4,14,768]{3,0,2,1:T(8,128)(2,1)}) %all-gather.5.cloned.1.call-update) | async-done | bytes 1376272 | tf_op jit(solution)/shard_map/all_gather | solution.py:70
  425.5 6.7 %fusion.33 = bf16[4,1024,16,14]{1,2,3,0:T(8,128)(2,1)S(1)} fusion(bf16[16,4,14,768]{3,0,2,1:T(8,128)(2,1)} %all-gather.5.cloned.1.call-done, bf16[4,768,1024]{2,1,0:T(8,128)(2,1)} %collective-permute-done.3, pred[]{:T(512)S(6)} %eq.124, bf16[1,4,768,1024]{3,2,1,0:T(8,128)(2,1)} %param.14), kind=kOutput, calls=%fused_computation.35 | convolution fusion | flops 1413349376 | bytes 15794177 | tf_op jit(solution)/shard_map/sjch,jhd->sjcd/dot_general | solution.py:71
  434.5 6.0 %all-to-all-start.3 = ((bf16[16,56,1024]{2,1,0:T(8,128)(2,1)}), bf16[16,56,1024]{2,1,0:T(8,128)(2,1)S(1)}, u32[]{:S(2)}, u32[]{:S(2)}) async-start(bf16[16,56,1024]{2,1,0:T(8,128)(2,1)} %copy.79), calls=%async_computation.5 | async-start | bytes 3670016 | tf_op jit(solution)/shard_map/all_to_all | solution.py:74
  441.3 40.0 %all-to-all-done.3 = bf16[16,56,1024]{2,1,0:T(8,128)(2,1)S(1)} async-done(((bf16[16,56,1024]{2,1,0:T(8,128)(2,1)}), bf16[16,56,1024]{2,1,0:T(8,128)(2,1)S(1)}, u32[]{:S(2)}, u32[]{:S(2)}) %all-to-all-start.3) | async-done | bytes 1835040 | tf_op jit(solution)/shard_map/all_to_all | solution.py:74
  487.9 4.2 multiply_reduce_fusion
  494.2 39.4 %psum.7 = f32[2]{0:T(128)S(1)} all-reduce(f32[2]{0:T(128)S(1)} %pad_maximum_fusion.2), channel_id=1, replica_groups=mesh['section'=2,'fsdp'=2,'expert'=8] {'section','fsdp','expert'}, use_global_device_ids=true, to_apply=%region_20.22 | all-reduce | flops 2 | bytes 16 | tf_op jit(solution)/shard_map/psum | solution.py:115
  (111 shorter events, 49.6 us)
Async XLA Ops:
  7.2 156.5 %reduce-scatter.3.cloned.1.call-start = ((), (), s32[]{:S(2)}) async-start(), calls=%async_computation.6 | async-start | bytes 8257536 | tf_op jit(solution)/shard_map/reduce_scatter | solution.py:66
  7.2 75.3 %collective-permute-start.4 = (bf16[4,1024,768]{2,1,0:T(8,128)(2,1)}, bf16[4,1024,768]{2,1,0:T(8,128)(2,1)}, u32[]{:S(2)}, u32[]{:S(2)}) collective-permute-start(bf16[4,1024,768]{2,1,0:T(8,128)(2,1)} %bitcast.187), channel_id=1, source_target_pairs={{0,16},{16,0},{1,17},{17,1},{2,18},{18,2},{3,19},{19,3},{4,20},{20... | collective-permute-start | bytes 18874376 | tf_op jit(solution)/shard_map/ppermute | solution.py:14
  8.5 9.4 %collective-permute-start = (s32[128,6]{0,1:T(8,128)S(1)}, s32[128,6]{0,1:T(8,128)S(1)}, u32[]{:S(2)}, u32[]{:S(2)}) collective-permute-start(s32[128,6]{0,1:T(8,128)S(1)} %bitcast.186), channel_id=1, source_target_pairs={{0,16},{16,0},{1,17},{17,1},{2,18},{18,2},{3,19},{19,3},{4,20},{20... | collective-permute-start | bytes 9224 | tf_op jit(solution)/shard_map/ppermute | solution.py:14
  8.5 12.2 %collective-permute-start.1 = (f32[2048]{0:T(1024)}, f32[2048]{0:T(1024)S(1)}, u32[]{:S(2)}, u32[]{:S(2)}) collective-permute-start(f32[2048]{0:T(1024)} %bitcast.184), channel_id=1, source_target_pairs={{0,16},{16,0},{1,17},{17,1},{2,18},{18,2},{3,19},{19,3},{4,20},{20... | collective-permute-start | bytes 24584 | tf_op jit(solution)/shard_map/ppermute | solution.py:14
  9.0 78.2 %collective-permute-start.5 = (bf16[4,1024,768]{2,1,0:T(8,128)(2,1)}, bf16[4,1024,768]{2,1,0:T(8,128)(2,1)}, u32[]{:S(2)}, u32[]{:S(2)}) collective-permute-start(bf16[4,1024,768]{2,1,0:T(8,128)(2,1)} %bitcast.188), channel_id=1, source_target_pairs={{0,16},{16,0},{1,17},{17,1},{2,18},{18,2},{3,19},{19,3},{4,20},{20... | collective-permute-start | bytes 18874376 | tf_op jit(solution)/shard_map/ppermute | solution.py:14
  94.8 97.1 %all-gather.3.cloned.1.call-start = ((), (), s32[]{:S(2)}) async-start(), calls=%async_computation.7 | async-start | bytes 2064384 | tf_op jit(solution)/shard_map/all_gather | solution.py:70
  95.0 71.7 %collective-permute-start.3 = (bf16[4,768,1024]{2,1,0:T(8,128)(2,1)}, bf16[4,768,1024]{2,1,0:T(8,128)(2,1)}, u32[]{:S(2)}, u32[]{:S(2)}) collective-permute-start(bf16[4,768,1024]{2,1,0:T(8,128)(2,1)} %bitcast.189), channel_id=1, source_target_pairs={{0,16},{16,0},{1,17},{17,1},{2,18},{18,2},{3,19},{19,3},{4,20},{20... | collective-permute-start | bytes 18874376 | tf_op jit(solution)/shard_map/ppermute | solution.py:14
  199.1 5.8 %copy-start.4 = (bf16[1,2048,32]{1,2,0:T(8,128)(2,1)S(1)}, bf16[1,2048,32]{1,2,0:T(8,128)(2,1)}, u32[]{:S(2)}) copy-start(bf16[1,2048,32]{1,2,0:T(8,128)(2,1)} %param.11) | copy-start | bytes 393220
  199.1 9.5 %copy-start.2 = (bf16[128,2048]{1,0:T(8,128)(2,1)S(1)}, bf16[128,2048]{1,0:T(8,128)(2,1)}, u32[]{:S(2)}) copy-start(bf16[128,2048]{1,0:T(8,128)(2,1)} %param.9) | copy-start | bytes 1572868
  199.1 49.1 %all-to-all-start.1 = ((bf16[16,56,1024]{2,1,0:T(8,128)(2,1)}), bf16[16,56,1024]{2,1,0:T(8,128)(2,1)S(1)}, u32[]{:S(2)}, u32[]{:S(2)}) async-start(bf16[16,56,1024]{2,1,0:T(8,128)(2,1)} %copy.68), calls=%async_computation.2 | async-start | bytes 3670016 | tf_op jit(solution)/shard_map/all_to_all | solution.py:74
  204.8 192.5 %reduce-scatter.5.cloned.1.call-start = ((), (), s32[]{:S(2)}) async-start(), calls=%async_computation.8 | async-start | bytes 8257536 | tf_op jit(solution)/shard_map/reduce_scatter | solution.py:66
  204.9 3.7 collective-permute-start.2
  208.6 42.0 %copy-start.6 = (bf16[2048,32]{0,1:T(8,128)(2,1)}, bf16[2048,32]{0,1:T(8,128)(2,1)S(1)}, u32[]{:S(2)}) copy-start(bf16[2048,32]{0,1:T(8,128)(2,1)S(1)} %collective-permute-done.2) | copy-start | bytes 393220
  253.1 5.8 %copy-start.3 = (bf16[128,2048]{1,0:T(8,128)(2,1)S(1)}, bf16[128,2048]{1,0:T(8,128)(2,1)}, u32[]{:S(2)}) copy-start(bf16[128,2048]{1,0:T(8,128)(2,1)} %param.9) | copy-start | bytes 1572868
  259.7 181.2 %copy-start = (bf16[64,2048]{1,0:T(8,128)(2,1)}, bf16[64,2048]{1,0:T(8,128)(2,1)S(1)}, u32[]{:S(2)}) copy-start(bf16[64,2048]{1,0:T(8,128)(2,1)S(1)} %get-tuple-element.13) | copy-start | bytes 786436
  331.0 94.5 %all-gather.5.cloned.1.call-start = ((), (), s32[]{:S(2)}) async-start(), calls=%async_computation.9 | async-start | bytes 2064384 | tf_op jit(solution)/shard_map/all_gather | solution.py:70
  434.5 6.4 %copy-start.5 = (bf16[1,2048,32]{1,2,0:T(8,128)(2,1)S(1)}, bf16[1,2048,32]{1,2,0:T(8,128)(2,1)}, u32[]{:S(2)}) copy-start(bf16[1,2048,32]{1,2,0:T(8,128)(2,1)} %param.11) | copy-start | bytes 393220
  434.5 6.4 %copy-start.7 = (bf16[2048,32]{0,1:T(8,128)(2,1)S(1)}, bf16[2048,32]{0,1:T(8,128)(2,1)}, u32[]{:S(2)}) copy-start(bf16[2048,32]{0,1:T(8,128)(2,1)} %copy-done.6) | copy-start | bytes 393220
  434.5 46.9 %all-to-all-start.3 = ((bf16[16,56,1024]{2,1,0:T(8,128)(2,1)}), bf16[16,56,1024]{2,1,0:T(8,128)(2,1)S(1)}, u32[]{:S(2)}, u32[]{:S(2)}) async-start(bf16[16,56,1024]{2,1,0:T(8,128)(2,1)} %copy.79), calls=%async_computation.5 | async-start | bytes 3670016 | tf_op jit(solution)/shard_map/all_to_all | solution.py:74
  486.2 5.9 %copy-start.1 = (bf16[64,2048]{1,0:T(8,128)(2,1)S(1)}, bf16[64,2048]{1,0:T(8,128)(2,1)}, u32[]{:S(2)}) copy-start(bf16[64,2048]{1,0:T(8,128)(2,1)} %copy-done) | copy-start | bytes 786436
  533.7 1.4 collective-permute-start.6
Sparse Core Ops, SparseCore 0:
  94.9 68.7 reduce-scatter.2
  166.9 24.9 all-gather.2
  331.1 66.1 reduce-scatter.4
  400.5 24.9 all-gather.4

commit v2 on v1

--- a/solution.py
+++ b/solution.py
@@ -12,6 +12,10 @@
 
 def other_section(value):
     return lax.ppermute(value, "section", [(0, 1), (1, 0)])
+
+
+def ring_pairs(count, shift):
+    return [(source, (source + shift) % count) for source in range(count)]
 
 
 def rms_scaled(hidden_rows, gain_row):
@@ -60,14 +64,33 @@
     )
     arrived = lax.all_to_all(outgoing, ("fsdp", "expert"), 0, 0, tiled=True)
     arrived = arrived.reshape(peers, local_experts, capacity, chunk)
+    fsdp_index = lax.axis_index("fsdp")
     gate_part = jnp.einsum("sjcd,jdh->sjch", arrived, gate_w, preferred_element_type=jnp.float32)
     up_part = jnp.einsum("sjcd,jdh->sjch", arrived, up_w, preferred_element_type=jnp.float32)
-    both = jnp.concatenate([gate_part, up_part], axis=-1)
-    summed = lax.psum_scatter(both, "fsdp", scatter_dimension=0, tiled=True)
-    gate_sum = summed[..., :hidden_units]
-    up_sum = summed[..., hidden_units:]
+    block_shape = (fsdp_count, expert_devices, local_experts, capacity, hidden_units)
+    gate_blocks = gate_part.reshape(block_shape)
+    up_blocks = up_part.reshape(block_shape)
+    gate_sum = lax.dynamic_index_in_dim(gate_blocks, fsdp_index, 0, keepdims=False)
+    up_sum = lax.dynamic_index_in_dim(up_blocks, fsdp_index, 0, keepdims=False)
+    for shift in range(1, fsdp_count):
+        target = (fsdp_index + shift) % fsdp_count
+        outgoing_pair = jnp.stack(
+            [
+                lax.dynamic_index_in_dim(gate_blocks, target, 0, keepdims=False),
+                lax.dynamic_index_in_dim(up_blocks, target, 0, keepdims=False),
+            ]
+        ).astype(jnp.bfloat16)
+        got = lax.ppermute(outgoing_pair, "fsdp", ring_pairs(fsdp_count, shift))
+        gate_sum = gate_sum + got[0].astype(jnp.float32)
+        up_sum = up_sum + got[1].astype(jnp.float32)
     inner_act = (jax.nn.silu(gate_sum) * up_sum).astype(jnp.bfloat16)
-    inner_all = lax.all_gather(inner_act, "fsdp", axis=0, tiled=True)
+    inner_pieces = [inner_act]
+    for shift in range(1, fsdp_count):
+        inner_pieces.append(lax.ppermute(inner_act, "fsdp", ring_pairs(fsdp_count, shift)))
+    order = (fsdp_index - jnp.arange(fsdp_count, dtype=jnp.int32)) % fsdp_count
+    inner_all = jnp.take(jnp.stack(inner_pieces), order, axis=0).reshape(
+        peers, local_experts, capacity, hidden_units
+    )
     produced = jnp.einsum(
         "sjch,jhd->sjcd", inner_all, down_w, preferred_element_type=jnp.float32
     ).astype(jnp.bfloat16)
@@ -112,7 +135,10 @@
         hidden = expert_layer(hidden, route_rows, gain_row, router_weight, weights, capacity)
         values = hidden.astype(jnp.float32)
         squares.append(jnp.sum(values * values))
-    totals = lax.psum(jnp.stack(squares), ("section", "fsdp", "expert"))
+    everyone = ("section", "fsdp", "expert")
+    device_count = sections * lax.axis_size("fsdp") * lax.axis_size("expert")
+    square_rows = jnp.broadcast_to(jnp.stack(squares)[None, :], (device_count, sections))
+    totals = jnp.sum(lax.all_to_all(square_rows, everyone, 0, 0, tiled=True), axis=0)
     token_total = token_rows * lax.axis_size("fsdp") * lax.axis_size("expert")
     stats = jnp.sqrt(totals / (token_total * width))
     layer_stats = lax.dynamic_slice_in_dim(stats, section_index, 1, 0)

time: 550 us -> 398 us (0.72)
  blocking collectives: 141 us -> 50.2 us
  waiting for transfers between devices: 271 us -> 213 us
  between operations: 14.7 us -> 1.49 us
  starting transfers between devices: 16.5 us -> 28.8 us
  other arithmetic: 29.4 us -> 23.2 us
    reduce_scatter x2 -> x0, waiting for transfers between devices: 133 us -> none  [expert_layer(): summed = lax.psum_scatter(both, 'fsdp', scatter_dimension=0, tiled=True)]
    ppermute x0 -> x4, waiting for transfers between devices: none -> 84 us  [the longest x2 59.6 us: expert_layer(): got = lax.ppermute(outgoing_pair, 'fsdp', ring_pairs(fsdp_count, shift))]
    all_to_all x2 -> x1, blocking collectives: 101 us -> 50.2 us  [expert_layer(): arrived = lax.all_to_all(outgoing, ('fsdp', 'expert'), 0, 0, tiled=True)]
    all_gather x2 -> x0, waiting for transfers between devices: 50.3 us -> none  [expert_layer(): inner_all = lax.all_gather(inner_act, 'fsdp', axis=0, tiled=True)]
    all_to_all x0 -> x2, waiting for transfers between devices: none -> 49.3 us  [the longest x1 42.6 us: expert_layer(): arrived = lax.all_to_all(outgoing, ('fsdp', 'expert'), 0, 0, tiled=True)]
    psum x1 -> x0, blocking collectives: 39.4 us -> none  [body(): totals = lax.psum(jnp.stack(squares), ('section', 'fsdp', 'expert'))]
    all_to_all x0 -> x2, starting transfers between devices: none -> 11.8 us  [the longest x1 8.75 us: expert_layer(): arrived = lax.all_to_all(outgoing, ('fsdp', 'expert'), 0, 0, tiled=True)]
    all_to_all x2, waiting for transfers between devices: 79.2 us -> 72.2 us  [expert_layer(): lax.all_to_all(produced.reshape(peers, local_experts * capacity, chunk),...]
  transfers between devices with their start and end apart: 13 -> 15, of which waited for: 8 -> 9; matrix products, arithmetic and copies ran while one was open for 5% -> 9% of each run, Pallas kernels for 0% -> 0%
where the time goes in v2:
time: 398 us; the launch traced here: 394 us
  waiting for transfers between devices  213 us (54%)
  blocking collectives  50.2 us (13%)
  matrix products  39.2 us (10%)
  local copies, waits for them, and re-layouts  37.7 us (9%)
  starting transfers between devices  28.8 us (7%)
  other arithmetic  23.2 us (6%)
    all_to_all x2, waiting for transfers between devices, expert_layer(): lax.all_to_all(produced.reshape(peers, local_experts * capacity, chunk),...  72.2 us
    ppermute x2, waiting for transfers between devices, expert_layer(): got = lax.ppermute(outgoing_pair, 'fsdp', ring_pairs(fsdp_count, shift))  59.6 us
    all_to_all x1, blocking collectives, expert_layer(): arrived = lax.all_to_all(outgoing, ('fsdp', 'expert'), 0, 0, tiled=True)  50.2 us
    all_to_all x1, waiting for transfers between devices, expert_layer(): arrived = lax.all_to_all(outgoing, ('fsdp', 'expert'), 0, 0, tiled=True)  42.6 us
    ppermute x2, waiting for transfers between devices, expert_layer(): lax.ppermute(inner_act, 'fsdp', ring_pairs(fsdp_count, shift))  24.3 us
    dot_general x2, matrix products, expert_layer(): jnp.einsum('sjcd,jdh->sjch', arrived, gate_w, preferred_element_type=jnp....  12.3 us
    dot_general x2, matrix products, expert_layer(): jnp.einsum('sjcd,jdh->sjch', arrived, up_w, preferred_element_type=jnp.fl...  11.6 us
    dot_general x2, matrix products, expert_layer(): jnp.einsum('sjch,jhd->sjcd', inner_all, down_w, preferred_element_type=jn...  11.1 us
  transfers between devices with their start and end apart: 15, of which 9 were waited for; matrix products, arithmetic and copies ran while one was open for 9% of the time, Pallas kernels for 0%

profile of v2, /device:TPU:0, one launch (start us, length us, event | category | flops | bytes accessed | tf_op | source)
XLA Modules:
  0.0 393.9 jit_solution(7090297111351584715)
XLA Ops:
  3.5 7.8 %collective-permute-done = s32[128,6]{0,1:T(8,128)S(1)} collective-permute-done((s32[128,6]{0,1:T(8,128)S(1)}, s32[128,6]{0,1:T(8,128)S(1)}, u32[]{:S(2)}, u32[]{:S(2)}) %collective-permute-start) | collective-permute-done | bytes 3104 | tf_op jit(solution)/shard_map/ppermute | solution.py:14
  14.9 2.9 convolution_convert_fusion.1
  17.8 4.6 %reshape.193 = bf16[8,56,2,1024]{3,2,1,0:T(2,128)(2,1)S(1)} reshape(bf16[448,2048]{1,0:T(8,128)(2,1)} %convolution_convert_fusion.1) | data formatting | bytes 3670016 | tf_op jit(solution)/shard_map/reshape | solution.py:61
  24.2 8.8 %all-to-all-start = ((bf16[16,56,1024]{2,1,0:T(8,128)(2,1)}), bf16[16,56,1024]{2,1,0:T(8,128)(2,1)S(1)}, u32[]{:S(2)}, u32[]{:S(2)}) async-start(bf16[16,56,1024]{2,1,0:T(8,128)(2,1)} %bitcast.252), calls=%async_computation | async-start | bytes 3670016 | tf_op jit(solution)/shard_map/all_to_all | solution.py:65
  33.1 42.6 %all-to-all-done = bf16[16,56,1024]{2,1,0:T(8,128)(2,1)S(1)} async-done(((bf16[16,56,1024]{2,1,0:T(8,128)(2,1)}), bf16[16,56,1024]{2,1,0:T(8,128)(2,1)S(1)}, u32[]{:S(2)}, u32[]{:S(2)}) %all-to-all-start) | async-done | bytes 1835040 | tf_op jit(solution)/shard_map/all_to_all | solution.py:65
  76.7 5.2 %fusion.30 = f32[2,8,4,14,768]{4,1,0,3,2:T(8,128)S(1)} fusion(bf16[16,4,14,1024]{3,0,2,1:T(8,128)(2,1)S(1)} %bitcast.256, bf16[4,1024,768]{2,1,0:T(8,128)(2,1)} %collective-permute-done.5, pred[]{:T(512)S(6)} %eq.115, bf16[1,4,1024,768]{3,2,1,0:T(8,128)(2,1)} %param.15), kind=kOutput, calls=%fused_computation.34 | convolution fusion | flops 1412431872 | bytes 17170432 | tf_op jit(solution)/shard_map/sjcd,jdh->sjch/dot_general | solution.py:69
  82.1 5.9 %fusion.27 = f32[2,8,4,14,768]{4,1,0,3,2:T(8,128)S(1)} fusion(bf16[16,4,14,1024]{3,0,2,1:T(8,128)(2,1)} %bitcast.257, bf16[4,1024,768]{2,1,0:T(8,128)(2,1)} %collective-permute-done.4, pred[]{:T(512)S(6)} %eq.115, bf16[1,4,1024,768]{3,2,1,0:T(8,128)(2,1)} %param.14), kind=kOutput, calls=%fused_computation.33 | convolution fusion | flops 1412431872 | bytes 17170432 | tf_op jit(solution)/shard_map/sjcd,jdh->sjch/dot_general | solution.py:68
  91.0 30.8 %collective-permute-done.6 = bf16[2,8,4,14,768]{4,1,0,3,2:T(8,128)(2,1)S(1)} collective-permute-done((bf16[2,8,4,14,768]{4,1,0,3,2:T(8,128)(2,1)S(1)}, bf16[2,8,4,14,768]{4,1,0,3,2:T(8,128)(2,1)S(1)}, u32[]{:S(2)}, u32[]{:S(2)}) %collective-permute-start.6) | collective-permute-done | bytes 1376288 | tf_op jit(solution)/shard_map/ppermute | solution.py:83
  127.6 14.5 %collective-permute-done.7 = bf16[8,4,14,768]{3,0,2,1:T(8,128)(2,1)S(1)} collective-permute-done((bf16[8,4,14,768]{3,0,2,1:T(8,128)(2,1)S(1)}, bf16[8,4,14,768]{3,0,2,1:T(8,128)(2,1)S(1)}, u32[]{:S(2)}, u32[]{:S(2)}) %collective-permute-start.7) | collective-permute-done | bytes 688160 | tf_op jit(solution)/shard_map/ppermute | solution.py:89
  142.9 4.6 %fusion.24 = bf16[4,1024,16,14]{1,2,3,0:T(8,128)(2,1)S(1)} fusion(bf16[4,768,1024]{2,1,0:T(8,128)(2,1)} %collective-permute-done.3, pred[]{:T(512)S(6)} %eq.115, bf16[1,4,768,1024]{3,2,1,0:T(8,128)(2,1)} %param.16, bf16[2,8,4,14,768]{4,1,3,2,0:T(8,128)(2,1)S(1)} %gather_fusion, pred[2]{0:T(512)(128)(4,1)S(1)} %compare_and_fusion.2), kind=kOutput, calls=%fused_computation.32 | convolution fusion | flops 1414037504 | bytes 15794179 | tf_op jit(solution)/shard_map/sjch,jhd->sjcd/dot_general | solution.py:94
  149.8 4.0 %all-to-all-start.1 = ((bf16[16,56,1024]{2,1,0:T(8,128)(2,1)}), bf16[16,56,1024]{2,1,0:T(8,128)(2,1)S(1)}, u32[]{:S(2)}, u32[]{:S(2)}) async-start(bf16[16,56,1024]{2,1,0:T(8,128)(2,1)} %copy.135), calls=%async_computation.1 | async-start | bytes 3670016 | tf_op jit(solution)/shard_map/all_to_all | solution.py:97
  158.4 37.5 %all-to-all-done.1 = bf16[16,56,1024]{2,1,0:T(8,128)(2,1)S(1)} async-done(((bf16[16,56,1024]{2,1,0:T(8,128)(2,1)}), bf16[16,56,1024]{2,1,0:T(8,128)(2,1)S(1)}, u32[]{:S(2)}, u32[]{:S(2)}) %all-to-all-start.1) | async-done | bytes 1835040 | tf_op jit(solution)/shard_map/all_to_all | solution.py:97
  202.4 4.3 %multiply_reduce_fusion.1 = f32[64,2048]{1,0:T(8,128)S(1)} fusion(bf16[64,6,2048]{2,1,0:T(8,128)(2,1)} %reshape.255, f32[64,6]{1,0:T(8,128)S(1)} %copy.123, pred[64,6]{1,0:T(8,128)(4,1)S(1)} %copy.128), kind=kLoop, calls=%fused_computation.29 | loop fusion | flops 3014656 | bytes 2099072 | tf_op jit(solution)/shard_map/reduce_sum | solution.py:110
  212.5 50.2 %all_to_all.26 = bf16[16,56,1024]{2,1,0:T(8,128)(2,1)S(1)} all-to-all(bf16[16,56,1024]{2,1,0:T(8,128)(2,1)S(1)} %bitcast.254), channel_id=1, replica_groups=mesh['section'=2,'fsdp'=2,'expert'=8] {'fsdp','expert'}, dimensions={0} | all-to-all | bytes 3670016 | tf_op jit(solution)/shard_map/all_to_all | solution.py:65
  263.7 6.4 %fusion.39 = f32[2,8,4,14,768]{4,1,0,3,2:T(8,128)S(1)} fusion(bf16[16,4,14,1024]{3,0,2,1:T(8,128)(2,1)S(1)} %bitcast.258, bf16[4,1024,768]{2,1,0:T(8,128)(2,1)} %collective-permute-done.5, pred[]{:T(512)S(6)} %eq.130, bf16[1,4,1024,768]{3,2,1,0:T(8,128)(2,1)} %param.15), kind=kOutput, calls=%fused_computation.37 | convolution fusion | flops 1412431872 | bytes 17170432 | tf_op jit(solution)/shard_map/sjcd,jdh->sjch/dot_general | solution.py:69
  270.2 6.4 %fusion.36 = f32[2,8,4,14,768]{4,1,0,3,2:T(8,128)S(1)} fusion(bf16[16,4,14,1024]{3,0,2,1:T(8,128)(2,1)S(1)} %bitcast.259, bf16[4,1024,768]{2,1,0:T(8,128)(2,1)} %collective-permute-done.4, pred[]{:T(512)S(6)} %eq.130, bf16[1,4,1024,768]{3,2,1,0:T(8,128)(2,1)} %param.14), kind=kOutput, calls=%fused_computation.36 | convolution fusion | flops 1412431872 | bytes 17170432 | tf_op jit(solution)/shard_map/sjcd,jdh->sjch/dot_general | solution.py:68
  277.8 28.8 %collective-permute-done.8 = bf16[2,8,4,14,768]{4,1,3,2,0:T(8,128)(2,1)S(1)} collective-permute-done((bf16[2,8,4,14,768]{4,1,3,2,0:T(8,128)(2,1)S(1)}, bf16[2,8,4,14,768]{4,1,3,2,0:T(8,128)(2,1)S(1)}, u32[]{:S(2)}, u32[]{:S(2)}) %collective-permute-start.8) | collective-permute-done | bytes 1376288 | tf_op jit(solution)/shard_map/ppermute | solution.py:83
  308.7 9.8 %collective-permute-done.9 = bf16[8,4,14,768]{3,0,2,1:T(8,128)(2,1)S(1)} collective-permute-done((bf16[8,4,14,768]{3,0,2,1:T(8,128)(2,1)S(1)}, bf16[8,4,14,768]{3,0,2,1:T(8,128)(2,1)S(1)}, u32[]{:S(2)}, u32[]{:S(2)}) %collective-permute-start.9) | collective-permute-done | bytes 688160 | tf_op jit(solution)/shard_map/ppermute | solution.py:89
  319.3 6.5 %fusion.33 = bf16[4,1024,16,14]{1,2,3,0:T(8,128)(2,1)S(1)} fusion(bf16[4,768,1024]{2,1,0:T(8,128)(2,1)} %collective-permute-done.3, pred[]{:T(512)S(6)} %eq.130, bf16[1,4,768,1024]{3,2,1,0:T(8,128)(2,1)} %param.16, bf16[2,8,4,14,768]{4,1,3,2,0:T(8,128)(2,1)S(1)} %gather_fusion.2, pred[2]{0:T(512)(128)(4,1)S(1)} %compare_and_fusion.2), kind=kOutput, calls=%fused_computation.35 | convolution fusion | flops 1414037504 | bytes 15794179 | tf_op jit(solution)/shard_map/sjch,jhd->sjcd/dot_general | solution.py:94
  328.1 4.9 %all-to-all-start.3 = ((bf16[16,56,1024]{2,1,0:T(8,128)(2,1)}), bf16[16,56,1024]{2,1,0:T(8,128)(2,1)S(1)}, u32[]{:S(2)}, u32[]{:S(2)}) async-start(bf16[16,56,1024]{2,1,0:T(8,128)(2,1)} %copy.151), calls=%async_computation.3 | async-start | bytes 3670016 | tf_op jit(solution)/shard_map/all_to_all | solution.py:97
  333.8 34.8 %all-to-all-done.3 = bf16[16,56,1024]{2,1,0:T(8,128)(2,1)S(1)} async-done(((bf16[16,56,1024]{2,1,0:T(8,128)(2,1)}), bf16[16,56,1024]{2,1,0:T(8,128)(2,1)S(1)}, u32[]{:S(2)}, u32[]{:S(2)}) %all-to-all-start.3) | async-done | bytes 1835040 | tf_op jit(solution)/shard_map/all_to_all | solution.py:97
  375.1 4.3 %multiply_reduce_fusion = f32[64,2048]{1,0:T(8,128)S(1)} fusion(bf16[64,6,2048]{2,1,0:T(8,128)(2,1)} %reshape.261, f32[64,6]{1,0:T(8,128)S(1)} %copy.138, pred[64,6]{1,0:T(8,128)(4,1)S(1)} %copy.143), kind=kLoop, calls=%fused_computation.28 | loop fusion | flops 3014656 | bytes 2099072 | tf_op jit(solution)/shard_map/reduce_sum | solution.py:110
  382.1 3.1 all-to-all-start.4
  385.5 6.7 %all-to-all-done.4 = f32[32,1,2]{2,1,0:T(1,128)S(1)} async-done(((f32[32,1,2]{2,1,0:T(1,128)}), f32[32,1,2]{2,1,0:T(1,128)S(1)}, u32[]{:S(2)}, u32[]{:S(2)}) %all-to-all-start.4) | async-done | bytes 288 | tf_op jit(solution)/shard_map/all_to_all | solution.py:141
  (132 shorter events, 57.1 us)
Async XLA Ops:
  0.6 76.1 %collective-permute-start.5 = (bf16[4,1024,768]{2,1,0:T(8,128)(2,1)}, bf16[4,1024,768]{2,1,0:T(8,128)(2,1)}, u32[]{:S(2)}, u32[]{:S(2)}) collective-permute-start(bf16[4,1024,768]{2,1,0:T(8,128)(2,1)} %bitcast.269), channel_id=1, source_target_pairs={{0,16},{16,0},{1,17},{17,1},{2,18},{18,2},{3,19},{19,3},{4,20},{20... | collective-permute-start | bytes 18874376 | tf_op jit(solution)/shard_map/ppermute | solution.py:14
  1.9 9.4 %collective-permute-start = (s32[128,6]{0,1:T(8,128)S(1)}, s32[128,6]{0,1:T(8,128)S(1)}, u32[]{:S(2)}, u32[]{:S(2)}) collective-permute-start(s32[128,6]{0,1:T(8,128)S(1)} %bitcast.268), channel_id=1, source_target_pairs={{0,16},{16,0},{1,17},{17,1},{2,18},{18,2},{3,19},{19,3},{4,20},{20... | collective-permute-start | bytes 9224 | tf_op jit(solution)/shard_map/ppermute | solution.py:14
  1.9 12.3 %collective-permute-start.1 = (f32[2048]{0:T(1024)}, f32[2048]{0:T(1024)S(1)}, u32[]{:S(2)}, u32[]{:S(2)}) collective-permute-start(f32[2048]{0:T(1024)} %bitcast.266), channel_id=1, source_target_pairs={{0,16},{16,0},{1,17},{17,1},{2,18},{18,2},{3,19},{19,3},{4,20},{20... | collective-permute-start | bytes 24584 | tf_op jit(solution)/shard_map/ppermute | solution.py:14
  2.4 79.7 %collective-permute-start.4 = (bf16[4,1024,768]{2,1,0:T(8,128)(2,1)}, bf16[4,1024,768]{2,1,0:T(8,128)(2,1)}, u32[]{:S(2)}, u32[]{:S(2)}) collective-permute-start(bf16[4,1024,768]{2,1,0:T(8,128)(2,1)} %bitcast.270), channel_id=1, source_target_pairs={{0,16},{16,0},{1,17},{17,1},{2,18},{18,2},{3,19},{19,3},{4,20},{20... | collective-permute-start | bytes 18874376 | tf_op jit(solution)/shard_map/ppermute | solution.py:14
  24.2 51.5 %all-to-all-start = ((bf16[16,56,1024]{2,1,0:T(8,128)(2,1)}), bf16[16,56,1024]{2,1,0:T(8,128)(2,1)S(1)}, u32[]{:S(2)}, u32[]{:S(2)}) async-start(bf16[16,56,1024]{2,1,0:T(8,128)(2,1)} %bitcast.252), calls=%async_computation | async-start | bytes 3670016 | tf_op jit(solution)/shard_map/all_to_all | solution.py:65
  33.0 109.9 %collective-permute-start.3 = (bf16[4,768,1024]{2,1,0:T(8,128)(2,1)}, bf16[4,768,1024]{2,1,0:T(8,128)(2,1)}, u32[]{:S(2)}, u32[]{:S(2)}) collective-permute-start(bf16[4,768,1024]{2,1,0:T(8,128)(2,1)} %bitcast.271), channel_id=1, source_target_pairs={{0,16},{16,0},{1,17},{17,1},{2,18},{18,2},{3,19},{19,3},{4,20},{20... | collective-permute-start | bytes 18874376 | tf_op jit(solution)/shard_map/ppermute | solution.py:14
  76.7 5.2 %copy-start.5 = (bf16[16,56,1024]{2,0,1:T(8,128)(2,1)}, bf16[16,56,1024]{2,0,1:T(8,128)(2,1)S(1)}, u32[]{:S(2)}) copy-start(bf16[16,56,1024]{2,0,1:T(8,128)(2,1)S(1)} %copy.130) | copy-start | bytes 5505028
  81.9 6.1 %copy-start = (f32[2,8,4,14,768]{4,1,0,3,2:T(8,128)}, f32[2,8,4,14,768]{4,1,0,3,2:T(8,128)S(1)}, u32[]{:S(2)}) copy-start(f32[2,8,4,14,768]{4,1,0,3,2:T(8,128)S(1)} %fusion.30) | copy-start | bytes 8257540
  89.6 32.3 %collective-permute-start.6 = (bf16[2,8,4,14,768]{4,1,0,3,2:T(8,128)(2,1)S(1)}, bf16[2,8,4,14,768]{4,1,0,3,2:T(8,128)(2,1)S(1)}, u32[]{:S(2)}, u32[]{:S(2)}) collective-permute-start(bf16[2,8,4,14,768]{4,1,0,3,2:T(8,128)(2,1)S(1)} %pad_maximum_fusion), channel_id=1, source_target_pairs={{0,8},{8,0},{1,9},{9,1},{2,10},{10,2},{3,11},{11,3},{4,12},{12,4},... | collective-permute-start | bytes 4128776 | tf_op jit(solution)/shard_map/ppermute | solution.py:83
  91.0 34.6 %copy-start.1 = (f32[2,8,4,14,768]{4,1,0,3,2:T(8,128)S(1)}, f32[2,8,4,14,768]{4,1,0,3,2:T(8,128)}, u32[]{:S(2)}) copy-start(f32[2,8,4,14,768]{4,1,0,3,2:T(8,128)} %copy-done) | copy-start | bytes 8257540
  124.1 18.0 %collective-permute-start.7 = (bf16[8,4,14,768]{3,0,2,1:T(8,128)(2,1)S(1)}, bf16[8,4,14,768]{3,0,2,1:T(8,128)(2,1)S(1)}, u32[]{:S(2)}, u32[]{:S(2)}) collective-permute-start(bf16[8,4,14,768]{3,0,2,1:T(8,128)(2,1)S(1)} %fusion.48), channel_id=1, source_target_pairs={{0,8},{8,0},{1,9},{9,1},{2,10},{10,2},{3,11},{11,3},{4,12},{12,4},... | collective-permute-start | bytes 2064392 | tf_op jit(solution)/shard_map/ppermute | solution.py:89
  149.8 8.2 %copy-start.6 = (bf16[128,2048]{1,0:T(8,128)(2,1)S(1)}, bf16[128,2048]{1,0:T(8,128)(2,1)}, u32[]{:S(2)}) copy-start(bf16[128,2048]{1,0:T(8,128)(2,1)} %param.11) | copy-start | bytes 1572868
  149.8 46.1 %all-to-all-start.1 = ((bf16[16,56,1024]{2,1,0:T(8,128)(2,1)}), bf16[16,56,1024]{2,1,0:T(8,128)(2,1)S(1)}, u32[]{:S(2)}, u32[]{:S(2)}) async-start(bf16[16,56,1024]{2,1,0:T(8,128)(2,1)} %copy.135), calls=%async_computation.1 | async-start | bytes 3670016 | tf_op jit(solution)/shard_map/all_to_all | solution.py:97
  153.8 4.2 %collective-permute-start.2 = (bf16[2048,32]{0,1:T(8,128)(2,1)S(1)}, bf16[2048,32]{0,1:T(8,128)(2,1)S(1)}, u32[]{:S(2)}, u32[]{:S(2)}) collective-permute-start(bf16[2048,32]{0,1:T(8,128)(2,1)S(1)} %bitcast.272), channel_id=1, source_target_pairs={{0,16},{16,0},{1,17},{17,1},{2,18},{18,2},{3,19},{19,3},{4,20},{20... | collective-permute-start | bytes 393224 | tf_op jit(solution)/shard_map/ppermute | solution.py:14
  158.0 39.8 %copy-start.10 = (bf16[2048,32]{0,1:T(8,128)(2,1)}, bf16[2048,32]{0,1:T(8,128)(2,1)S(1)}, u32[]{:S(2)}) copy-start(bf16[2048,32]{0,1:T(8,128)(2,1)S(1)} %collective-permute-done.2) | copy-start | bytes 393220
  202.4 4.3 %copy-start.7 = (bf16[128,2048]{1,0:T(8,128)(2,1)S(1)}, bf16[128,2048]{1,0:T(8,128)(2,1)}, u32[]{:S(2)}) copy-start(bf16[128,2048]{1,0:T(8,128)(2,1)} %param.11) | copy-start | bytes 1572868
  207.4 125.9 %copy-start.3 = (bf16[64,2048]{1,0:T(8,128)(2,1)}, bf16[64,2048]{1,0:T(8,128)(2,1)S(1)}, u32[]{:S(2)}) copy-start(bf16[64,2048]{1,0:T(8,128)(2,1)S(1)} %get-tuple-element.14) | copy-start | bytes 786436
  276.8 29.8 %collective-permute-start.8 = (bf16[2,8,4,14,768]{4,1,3,2,0:T(8,128)(2,1)S(1)}, bf16[2,8,4,14,768]{4,1,3,2,0:T(8,128)(2,1)S(1)}, u32[]{:S(2)}, u32[]{:S(2)}) collective-permute-start(bf16[2,8,4,14,768]{4,1,3,2,0:T(8,128)(2,1)S(1)} %pad_maximum_fusion.2), channel_id=1, source_target_pairs={{0,8},{8,0},{1,9},{9,1},{2,10},{10,2},{3,11},{11,3},{4,12},{12,4},... | collective-permute-start | bytes 4128776 | tf_op jit(solution)/shard_map/ppermute | solution.py:83
  307.2 11.4 %collective-permute-start.9 = (bf16[8,4,14,768]{3,0,2,1:T(8,128)(2,1)S(1)}, bf16[8,4,14,768]{3,0,2,1:T(8,128)(2,1)S(1)}, u32[]{:S(2)}, u32[]{:S(2)}) collective-permute-start(bf16[8,4,14,768]{3,0,2,1:T(8,128)(2,1)S(1)} %fusion.43), channel_id=1, source_target_pairs={{0,8},{8,0},{1,9},{9,1},{2,10},{10,2},{3,11},{11,3},{4,12},{12,4},... | collective-permute-start | bytes 2064392 | tf_op jit(solution)/shard_map/ppermute | solution.py:89
  328.1 5.3 %copy-start.9 = (bf16[1,2048,32]{1,2,0:T(8,128)(2,1)S(1)}, bf16[1,2048,32]{1,2,0:T(8,128)(2,1)}, u32[]{:S(2)}) copy-start(bf16[1,2048,32]{1,2,0:T(8,128)(2,1)} %param.13) | copy-start | bytes 393220
  328.1 5.3 %copy-start.11 = (bf16[2048,32]{0,1:T(8,128)(2,1)S(1)}, bf16[2048,32]{0,1:T(8,128)(2,1)}, u32[]{:S(2)}) copy-start(bf16[2048,32]{0,1:T(8,128)(2,1)} %copy-done.10) | copy-start | bytes 393220
  328.1 40.5 %all-to-all-start.3 = ((bf16[16,56,1024]{2,1,0:T(8,128)(2,1)}), bf16[16,56,1024]{2,1,0:T(8,128)(2,1)S(1)}, u32[]{:S(2)}, u32[]{:S(2)}) async-start(bf16[16,56,1024]{2,1,0:T(8,128)(2,1)} %copy.151), calls=%async_computation.3 | async-start | bytes 3670016 | tf_op jit(solution)/shard_map/all_to_all | solution.py:97
  382.1 10.2 %all-to-all-start.4 = ((f32[32,1,2]{2,1,0:T(1,128)}), f32[32,1,2]{2,1,0:T(1,128)S(1)}, u32[]{:S(2)}, u32[]{:S(2)}) async-start(f32[32,1,2]{2,1,0:T(1,128)} %broadcast_in_dim.20), calls=%async_computation.4 | async-start | bytes 32768 | tf_op jit(solution)/shard_map/all_to_all | solution.py:141
  385.2 7.7 %collective-permute-start.10 = (bf16[64,1024]{1,0:T(8,128)(2,1)S(1)}, bf16[64,1024]{1,0:T(8,128)(2,1)S(1)}, u32[]{:S(2)}, u32[]{:S(2)}) collective-permute-start(bf16[64,1024]{1,0:T(8,128)(2,1)S(1)} %get-tuple-element.18), channel_id=1, source_target_pairs={{0,16},{16,0},{1,17},{17,1},{2,18},{18,2},{3,19},{19,3},{4,20},{20... | collective-permute-start | bytes 393224 | tf_op jit(solution)/shard_map/ppermute | solution.py:14
  (3 other events, 9.9 us)

commit v3 on v2

--- a/solution.py
+++ b/solution.py
@@ -55,13 +55,15 @@
     mix_weights = gate_weights(normed, router_weight, route_rows)
     positions = slot_positions(route_rows, experts_count, capacity)
     slot_ids = jnp.arange(experts_count * capacity, dtype=jnp.int32)
-    placing = jnp.any(positions[None, :, :] == slot_ids[:, None, None], axis=2).astype(jnp.bfloat16)
-    buffer = jnp.dot(placing, normed, preferred_element_type=jnp.float32).astype(jnp.bfloat16)
-    outgoing = (
-        buffer.reshape(expert_devices, local_experts * capacity, fsdp_count, chunk)
-        .transpose(2, 0, 1, 3)
-        .reshape(peers, local_experts * capacity, chunk)
-    )
+    hits = positions[:, :, None] == slot_ids[None, None, :]
+    placing = jnp.any(hits, axis=1).astype(jnp.bfloat16)
+    buffer = jnp.einsum(
+        "rs,rfd->fsd",
+        placing,
+        normed.reshape(normed.shape[0], fsdp_count, chunk),
+        preferred_element_type=jnp.float32,
+    ).astype(jnp.bfloat16)
+    outgoing = buffer.reshape(peers, local_experts * capacity, chunk)
     arrived = lax.all_to_all(outgoing, ("fsdp", "expert"), 0, 0, tiled=True)
     arrived = arrived.reshape(peers, local_experts, capacity, chunk)
     fsdp_index = lax.axis_index("fsdp")
@@ -101,13 +103,14 @@
         0,
         tiled=True,
     )
-    flat_out = (
-        returned.reshape(fsdp_count, expert_devices, local_experts * capacity, chunk)
-        .transpose(1, 2, 0, 3)
-        .reshape(experts_count * capacity, width)
-    )
-    picked = jnp.take(flat_out, positions, axis=0)
-    branch_sum = jnp.sum(mix_weights[:, :, None] * picked.astype(jnp.float32), axis=1)
+    combining = jnp.sum(jnp.where(hits, mix_weights[:, :, None], 0.0), axis=1)
+    branch_sum = jnp.einsum(
+        "rs,fsd->rfd",
+        combining,
+        returned.reshape(fsdp_count, experts_count * capacity, chunk).astype(jnp.float32),
+        precision=lax.Precision.HIGHEST,
+        preferred_element_type=jnp.float32,
+    ).reshape(normed.shape[0], width)
     return (entering.astype(jnp.float32) + branch_sum).astype(jnp.bfloat16)
 
 

time: 398 us -> 364 us (0.915)
  local copies, waits for them, and re-layouts: 37.7 us -> 14.3 us
  other arithmetic: 23.2 us -> 13.8 us
    reshape x6 -> x0, local copies, waits for them, and re-layouts: 14.4 us -> none  [the longest x4 10.7 us: expert_layer(): buffer.reshape(expert_devices, local_experts * capacity, fsdp_count, chunk)]
    reduce_sum x4 -> x2, other arithmetic: 10.1 us -> 0.35 us  [expert_layer(): combining = jnp.sum(jnp.where(hits, mix_weights[:, :, None], 0.0), axis=1)]
    gather x4 -> x0, local copies, waits for them, and re-layouts: 8.11 us -> none  [expert_layer(): picked = jnp.take(flat_out, positions, axis=0)]
  transfers between devices with their start and end apart: 15 -> 15, of which waited for: 9 -> 10; matrix products, arithmetic and copies ran while one was open for 9% -> 8% of each run, Pallas kernels for 0% -> 0%
where the time goes in v3:
time: 364 us; the launch traced here: 363 us
  waiting for transfers between devices  215 us (59%)
  blocking collectives  49.6 us (14%)
  matrix products  41.4 us (11%)
  starting transfers between devices  27.9 us (8%)
  local copies, waits for them, and re-layouts  14.3 us (4%)
  other arithmetic  13.8 us (4%)
    all_to_all x2, waiting for transfers between devices, expert_layer(): lax.all_to_all(produced.reshape(peers, local_experts * capacity, chunk),...  73.8 us
    ppermute x2, waiting for transfers between devices, expert_layer(): got = lax.ppermute(outgoing_pair, 'fsdp', ring_pairs(fsdp_count, shift))  59.6 us
    all_to_all x1, blocking collectives, expert_layer(): arrived = lax.all_to_all(outgoing, ('fsdp', 'expert'), 0, 0, tiled=True)  49.6 us
    all_to_all x1, waiting for transfers between devices, expert_layer(): arrived = lax.all_to_all(outgoing, ('fsdp', 'expert'), 0, 0, tiled=True)  42.6 us
    ppermute x2, waiting for transfers between devices, expert_layer(): lax.ppermute(inner_act, 'fsdp', ring_pairs(fsdp_count, shift))  24.2 us
    dot_general x2, matrix products, expert_layer(): jnp.einsum('sjcd,jdh->sjch', arrived, gate_w, preferred_element_type=jnp....  12.3 us
    dot_general x2, matrix products, expert_layer(): jnp.einsum('sjcd,jdh->sjch', arrived, up_w, preferred_element_type=jnp.fl...  11.5 us
    dot_general x2, matrix products, expert_layer(): jnp.einsum('sjch,jhd->sjcd', inner_all, down_w, preferred_element_type=jn...  11.1 us
  transfers between devices with their start and end apart: 15, of which 10 were waited for; matrix products, arithmetic and copies ran while one was open for 8% of the time, Pallas kernels for 0%

profile of v3, /device:TPU:0, one launch (start us, length us, event | category | flops | bytes accessed | tf_op | source)
XLA Modules:
  0.0 363.4 jit_solution(10987006965500392779)
XLA Ops:
  3.7 7.6 %collective-permute-done = s32[128,6]{1,0:T(8,128)S(1)} collective-permute-done((s32[128,6]{1,0:T(8,128)S(1)}, s32[128,6]{1,0:T(8,128)S(1)}, u32[]{:S(2)}, u32[]{:S(2)}) %collective-permute-start) | collective-permute-done | bytes 3104 | tf_op jit(solution)/shard_map/ppermute | solution.py:14
  16.8 1.9 convolution_convert_fusion.1
  18.7 8.2 %all-to-all-start = ((bf16[16,56,1024]{2,1,0:T(8,128)(2,1)}), bf16[16,56,1024]{2,1,0:T(8,128)(2,1)S(1)}, u32[]{:S(2)}, u32[]{:S(2)}) async-start(bf16[16,56,1024]{2,1,0:T(8,128)(2,1)} %bitcast.262), calls=%async_computation | async-start | bytes 3670016 | tf_op jit(solution)/shard_map/all_to_all | solution.py:67
  27.0 42.6 %all-to-all-done = bf16[16,56,1024]{2,1,0:T(8,128)(2,1)S(1)} async-done(((bf16[16,56,1024]{2,1,0:T(8,128)(2,1)}), bf16[16,56,1024]{2,1,0:T(8,128)(2,1)S(1)}, u32[]{:S(2)}, u32[]{:S(2)}) %all-to-all-start) | async-done | bytes 1835040 | tf_op jit(solution)/shard_map/all_to_all | solution.py:67
  70.7 5.2 %fusion.33 = f32[2,8,4,14,768]{4,1,0,3,2:T(8,128)S(1)} fusion(bf16[16,4,14,1024]{3,0,2,1:T(8,128)(2,1)S(1)} %bitcast.266, bf16[4,1024,768]{2,1,0:T(8,128)(2,1)} %collective-permute-done.5, pred[]{:T(512)S(6)} %eq.115, bf16[1,4,1024,768]{3,2,1,0:T(8,128)(2,1)} %param.13), kind=kOutput, calls=%fused_computation.35 | convolution fusion | flops 1412431872 | bytes 17170432 | tf_op jit(solution)/shard_map/sjcd,jdh->sjch/dot_general | solution.py:71
  76.0 5.9 %fusion.30 = f32[2,8,4,14,768]{4,1,0,3,2:T(8,128)S(1)} fusion(bf16[16,4,14,1024]{3,0,2,1:T(8,128)(2,1)} %bitcast.267, bf16[4,1024,768]{2,1,0:T(8,128)(2,1)} %collective-permute-done.4, pred[]{:T(512)S(6)} %eq.115, bf16[1,4,1024,768]{3,2,1,0:T(8,128)(2,1)} %param.12), kind=kOutput, calls=%fused_computation.34 | convolution fusion | flops 1412431872 | bytes 17170432 | tf_op jit(solution)/shard_map/sjcd,jdh->sjch/dot_general | solution.py:70
  85.0 30.8 %collective-permute-done.6 = bf16[2,8,4,14,768]{4,1,0,3,2:T(8,128)(2,1)S(1)} collective-permute-done((bf16[2,8,4,14,768]{4,1,0,3,2:T(8,128)(2,1)S(1)}, bf16[2,8,4,14,768]{4,1,0,3,2:T(8,128)(2,1)S(1)}, u32[]{:S(2)}, u32[]{:S(2)}) %collective-permute-start.6) | collective-permute-done | bytes 1376288 | tf_op jit(solution)/shard_map/ppermute | solution.py:85
  115.9 2.2 fusion.51
  121.6 14.5 %collective-permute-done.7 = bf16[8,4,14,768]{3,0,2,1:T(8,128)(2,1)S(1)} collective-permute-done((bf16[8,4,14,768]{3,0,2,1:T(8,128)(2,1)S(1)}, bf16[8,4,14,768]{3,0,2,1:T(8,128)(2,1)S(1)}, u32[]{:S(2)}, u32[]{:S(2)}) %collective-permute-start.7) | collective-permute-done | bytes 688160 | tf_op jit(solution)/shard_map/ppermute | solution.py:91
  136.8 4.6 %fusion.27 = bf16[4,1024,16,14]{1,2,3,0:T(8,128)(2,1)S(1)} fusion(bf16[4,768,1024]{2,1,0:T(8,128)(2,1)} %collective-permute-done.3, pred[]{:T(512)S(6)} %eq.115, bf16[1,4,768,1024]{3,2,1,0:T(8,128)(2,1)} %param.14, bf16[2,8,4,14,768]{4,1,3,2,0:T(8,128)(2,1)S(1)} %gather_fusion, pred[2]{0:T(512)(128)(4,1)S(1)} %compare_and_fusion), kind=kOutput, calls=%fused_computation.33 | convolution fusion | flops 1414037504 | bytes 15794179 | tf_op jit(solution)/shard_map/sjch,jhd->sjcd/dot_general | solution.py:96
  141.5 2.3 copy.84
  143.7 4.1 %all-to-all-start.1 = ((bf16[16,56,1024]{2,1,0:T(8,128)(2,1)}), bf16[16,56,1024]{2,1,0:T(8,128)(2,1)S(1)}, u32[]{:S(2)}, u32[]{:S(2)}) async-start(bf16[16,56,1024]{2,1,0:T(8,128)(2,1)} %copy.84), calls=%async_computation.1 | async-start | bytes 3670016 | tf_op jit(solution)/shard_map/all_to_all | solution.py:99
  150.9 39.2 %all-to-all-done.1 = bf16[16,56,1024]{2,1,0:T(8,128)(2,1)S(1)} async-done(((bf16[16,56,1024]{2,1,0:T(8,128)(2,1)}), bf16[16,56,1024]{2,1,0:T(8,128)(2,1)S(1)}, u32[]{:S(2)}, u32[]{:S(2)}) %all-to-all-start.1) | async-done | bytes 1835040 | tf_op jit(solution)/shard_map/all_to_all | solution.py:99
  193.7 49.6 %all_to_all.26 = bf16[16,56,1024]{2,1,0:T(8,128)(2,1)S(1)} all-to-all(bf16[16,56,1024]{2,1,0:T(8,128)(2,1)S(1)} %bitcast.265), channel_id=1, replica_groups=mesh['section'=2,'fsdp'=2,'expert'=8] {'fsdp','expert'}, dimensions={0} | all-to-all | bytes 3670016 | tf_op jit(solution)/shard_map/all_to_all | solution.py:67
  244.3 6.3 %fusion.42 = f32[2,8,4,14,768]{4,1,0,3,2:T(8,128)S(1)} fusion(bf16[16,4,14,1024]{3,0,2,1:T(8,128)(2,1)S(1)} %bitcast.268, bf16[4,1024,768]{2,1,0:T(8,128)(2,1)} %collective-permute-done.5, pred[]{:T(512)S(6)} %eq.130, bf16[1,4,1024,768]{3,2,1,0:T(8,128)(2,1)} %param.13), kind=kOutput, calls=%fused_computation.38 | convolution fusion | flops 1412431872 | bytes 17170432 | tf_op jit(solution)/shard_map/sjcd,jdh->sjch/dot_general | solution.py:71
  250.7 6.3 %fusion.39 = f32[2,8,4,14,768]{4,1,0,3,2:T(8,128)S(1)} fusion(bf16[16,4,14,1024]{3,0,2,1:T(8,128)(2,1)S(1)} %bitcast.269, bf16[4,1024,768]{2,1,0:T(8,128)(2,1)} %collective-permute-done.4, pred[]{:T(512)S(6)} %eq.130, bf16[1,4,1024,768]{3,2,1,0:T(8,128)(2,1)} %param.12), kind=kOutput, calls=%fused_computation.37 | convolution fusion | flops 1412431872 | bytes 17170432 | tf_op jit(solution)/shard_map/sjcd,jdh->sjch/dot_general | solution.py:70
  258.3 28.8 %collective-permute-done.8 = bf16[2,8,4,14,768]{4,1,3,2,0:T(8,128)(2,1)S(1)} collective-permute-done((bf16[2,8,4,14,768]{4,1,3,2,0:T(8,128)(2,1)S(1)}, bf16[2,8,4,14,768]{4,1,3,2,0:T(8,128)(2,1)S(1)}, u32[]{:S(2)}, u32[]{:S(2)}) %collective-permute-start.8) | collective-permute-done | bytes 1376288 | tf_op jit(solution)/shard_map/ppermute | solution.py:85
  289.2 9.7 %collective-permute-done.9 = bf16[8,4,14,768]{3,0,2,1:T(8,128)(2,1)S(1)} collective-permute-done((bf16[8,4,14,768]{3,0,2,1:T(8,128)(2,1)S(1)}, bf16[8,4,14,768]{3,0,2,1:T(8,128)(2,1)S(1)}, u32[]{:S(2)}, u32[]{:S(2)}) %collective-permute-start.9) | collective-permute-done | bytes 688160 | tf_op jit(solution)/shard_map/ppermute | solution.py:91
  299.7 6.5 %fusion.36 = bf16[4,1024,16,14]{1,2,3,0:T(8,128)(2,1)S(1)} fusion(bf16[4,768,1024]{2,1,0:T(8,128)(2,1)} %collective-permute-done.3, pred[]{:T(512)S(6)} %eq.130, bf16[1,4,768,1024]{3,2,1,0:T(8,128)(2,1)} %param.14, bf16[2,8,4,14,768]{4,1,3,2,0:T(8,128)(2,1)S(1)} %gather_fusion.1, pred[2]{0:T(512)(128)(4,1)S(1)} %compare_and_fusion), kind=kOutput, calls=%fused_computation.36 | convolution fusion | flops 1414037504 | bytes 15794179 | tf_op jit(solution)/shard_map/sjch,jhd->sjcd/dot_general | solution.py:96
  306.2 2.3 copy.96
  308.4 4.4 %all-to-all-start.3 = ((bf16[16,56,1024]{2,1,0:T(8,128)(2,1)}), bf16[16,56,1024]{2,1,0:T(8,128)(2,1)S(1)}, u32[]{:S(2)}, u32[]{:S(2)}) async-start(bf16[16,56,1024]{2,1,0:T(8,128)(2,1)} %copy.96), calls=%async_computation.3 | async-start | bytes 3670016 | tf_op jit(solution)/shard_map/all_to_all | solution.py:99
  313.4 34.6 %all-to-all-done.3 = bf16[16,56,1024]{2,1,0:T(8,128)(2,1)S(1)} async-done(((bf16[16,56,1024]{2,1,0:T(8,128)(2,1)}), bf16[16,56,1024]{2,1,0:T(8,128)(2,1)S(1)}, u32[]{:S(2)}, u32[]{:S(2)}) %all-to-all-start.3) | async-done | bytes 1835040 | tf_op jit(solution)/shard_map/all_to_all | solution.py:99
  351.8 3.1 all-to-all-start.4
  355.2 6.7 %all-to-all-done.4 = f32[32,1,2]{2,1,0:T(1,128)S(1)} async-done(((f32[32,1,2]{2,1,0:T(1,128)}), f32[32,1,2]{2,1,0:T(1,128)S(1)}, u32[]{:S(2)}, u32[]{:S(2)}) %all-to-all-start.4) | async-done | bytes 288 | tf_op jit(solution)/shard_map/all_to_all | solution.py:144
  (108 shorter events, 34.7 us)
Async XLA Ops:
  0.6 70.1 %collective-permute-start.5 = (bf16[4,1024,768]{2,1,0:T(8,128)(2,1)}, bf16[4,1024,768]{2,1,0:T(8,128)(2,1)}, u32[]{:S(2)}, u32[]{:S(2)}) collective-permute-start(bf16[4,1024,768]{2,1,0:T(8,128)(2,1)} %bitcast.282), channel_id=1, source_target_pairs={{0,16},{16,0},{1,17},{17,1},{2,18},{18,2},{3,19},{19,3},{4,20},{20... | collective-permute-start | bytes 18874376 | tf_op jit(solution)/shard_map/ppermute | solution.py:14
  2.0 9.3 %collective-permute-start = (s32[128,6]{1,0:T(8,128)S(1)}, s32[128,6]{1,0:T(8,128)S(1)}, u32[]{:S(2)}, u32[]{:S(2)}) collective-permute-start(s32[128,6]{1,0:T(8,128)S(1)} %bitcast.276), channel_id=1, source_target_pairs={{0,16},{16,0},{1,17},{17,1},{2,18},{18,2},{3,19},{19,3},{4,20},{20... | collective-permute-start | bytes 9224 | tf_op jit(solution)/shard_map/ppermute | solution.py:14
  2.1 12.9 %collective-permute-start.1 = (f32[2048]{0:T(1024)}, f32[2048]{0:T(1024)S(1)}, u32[]{:S(2)}, u32[]{:S(2)}) collective-permute-start(f32[2048]{0:T(1024)} %bitcast.280), channel_id=1, source_target_pairs={{0,16},{16,0},{1,17},{17,1},{2,18},{18,2},{3,19},{19,3},{4,20},{20... | collective-permute-start | bytes 24584 | tf_op jit(solution)/shard_map/ppermute | solution.py:14
  2.5 73.5 %collective-permute-start.4 = (bf16[4,1024,768]{2,1,0:T(8,128)(2,1)}, bf16[4,1024,768]{2,1,0:T(8,128)(2,1)}, u32[]{:S(2)}, u32[]{:S(2)}) collective-permute-start(bf16[4,1024,768]{2,1,0:T(8,128)(2,1)} %bitcast.283), channel_id=1, source_target_pairs={{0,16},{16,0},{1,17},{17,1},{2,18},{18,2},{3,19},{19,3},{4,20},{20... | collective-permute-start | bytes 18874376 | tf_op jit(solution)/shard_map/ppermute | solution.py:14
  11.3 7.4 %copy-start.5 = (s32[64,6]{1,0:T(8,128)}, s32[64,6]{1,0:T(8,128)S(1)}, u32[]{:S(2)}) copy-start(s32[64,6]{1,0:T(8,128)S(1)} %get-tuple-element.11) | copy-start | bytes 4612
  18.7 51.0 %all-to-all-start = ((bf16[16,56,1024]{2,1,0:T(8,128)(2,1)}), bf16[16,56,1024]{2,1,0:T(8,128)(2,1)S(1)}, u32[]{:S(2)}, u32[]{:S(2)}) async-start(bf16[16,56,1024]{2,1,0:T(8,128)(2,1)} %bitcast.262), calls=%async_computation | async-start | bytes 3670016 | tf_op jit(solution)/shard_map/all_to_all | solution.py:67
  26.9 109.9 %collective-permute-start.3 = (bf16[4,768,1024]{2,1,0:T(8,128)(2,1)}, bf16[4,768,1024]{2,1,0:T(8,128)(2,1)}, u32[]{:S(2)}, u32[]{:S(2)}) collective-permute-start(bf16[4,768,1024]{2,1,0:T(8,128)(2,1)} %bitcast.284), channel_id=1, source_target_pairs={{0,16},{16,0},{1,17},{17,1},{2,18},{18,2},{3,19},{19,3},{4,20},{20... | collective-permute-start | bytes 18874376 | tf_op jit(solution)/shard_map/ppermute | solution.py:14
  70.7 5.2 %copy-start.3 = (bf16[16,56,1024]{2,0,1:T(8,128)(2,1)}, bf16[16,56,1024]{2,0,1:T(8,128)(2,1)S(1)}, u32[]{:S(2)}) copy-start(bf16[16,56,1024]{2,0,1:T(8,128)(2,1)S(1)} %copy.79) | copy-start | bytes 5505028
  75.9 6.0 %copy-start = (f32[2,8,4,14,768]{4,1,0,3,2:T(8,128)}, f32[2,8,4,14,768]{4,1,0,3,2:T(8,128)S(1)}, u32[]{:S(2)}) copy-start(f32[2,8,4,14,768]{4,1,0,3,2:T(8,128)S(1)} %fusion.33) | copy-start | bytes 8257540
  83.6 32.3 %collective-permute-start.6 = (bf16[2,8,4,14,768]{4,1,0,3,2:T(8,128)(2,1)S(1)}, bf16[2,8,4,14,768]{4,1,0,3,2:T(8,128)(2,1)S(1)}, u32[]{:S(2)}, u32[]{:S(2)}) collective-permute-start(bf16[2,8,4,14,768]{4,1,0,3,2:T(8,128)(2,1)S(1)} %pad_maximum_fusion), channel_id=1, source_target_pairs={{0,8},{8,0},{1,9},{9,1},{2,10},{10,2},{3,11},{11,3},{4,12},{12,4},... | collective-permute-start | bytes 4128776 | tf_op jit(solution)/shard_map/ppermute | solution.py:85
  85.0 34.6 %copy-start.1 = (f32[2,8,4,14,768]{4,1,0,3,2:T(8,128)S(1)}, f32[2,8,4,14,768]{4,1,0,3,2:T(8,128)}, u32[]{:S(2)}) copy-start(f32[2,8,4,14,768]{4,1,0,3,2:T(8,128)} %copy-done) | copy-start | bytes 8257540
  118.1 18.0 %collective-permute-start.7 = (bf16[8,4,14,768]{3,0,2,1:T(8,128)(2,1)S(1)}, bf16[8,4,14,768]{3,0,2,1:T(8,128)(2,1)S(1)}, u32[]{:S(2)}, u32[]{:S(2)}) collective-permute-start(bf16[8,4,14,768]{3,0,2,1:T(8,128)(2,1)S(1)} %fusion.51), channel_id=1, source_target_pairs={{0,8},{8,0},{1,9},{9,1},{2,10},{10,2},{3,11},{11,3},{4,12},{12,4},... | collective-permute-start | bytes 2064392 | tf_op jit(solution)/shard_map/ppermute | solution.py:91
  143.7 4.1 %copy-start.7 = (bf16[1,2048,32]{1,2,0:T(8,128)(2,1)S(1)}, bf16[1,2048,32]{1,2,0:T(8,128)(2,1)}, u32[]{:S(2)}) copy-start(bf16[1,2048,32]{1,2,0:T(8,128)(2,1)} %param.11) | copy-start | bytes 393220
  143.7 46.3 %all-to-all-start.1 = ((bf16[16,56,1024]{2,1,0:T(8,128)(2,1)}), bf16[16,56,1024]{2,1,0:T(8,128)(2,1)S(1)}, u32[]{:S(2)}, u32[]{:S(2)}) async-start(bf16[16,56,1024]{2,1,0:T(8,128)(2,1)} %copy.84), calls=%async_computation.1 | async-start | bytes 3670016 | tf_op jit(solution)/shard_map/all_to_all | solution.py:99
  147.8 2.6 collective-permute-start.2
  150.4 39.8 %copy-start.9 = (bf16[2048,32]{0,1:T(8,128)(2,1)}, bf16[2048,32]{0,1:T(8,128)(2,1)S(1)}, u32[]{:S(2)}) copy-start(bf16[2048,32]{0,1:T(8,128)(2,1)S(1)} %collective-permute-done.2) | copy-start | bytes 393220
  257.3 29.8 %collective-permute-start.8 = (bf16[2,8,4,14,768]{4,1,3,2,0:T(8,128)(2,1)S(1)}, bf16[2,8,4,14,768]{4,1,3,2,0:T(8,128)(2,1)S(1)}, u32[]{:S(2)}, u32[]{:S(2)}) collective-permute-start(bf16[2,8,4,14,768]{4,1,3,2,0:T(8,128)(2,1)S(1)} %pad_maximum_fusion.2), channel_id=1, source_target_pairs={{0,8},{8,0},{1,9},{9,1},{2,10},{10,2},{3,11},{11,3},{4,12},{12,4},... | collective-permute-start | bytes 4128776 | tf_op jit(solution)/shard_map/ppermute | solution.py:85
  287.7 11.3 %collective-permute-start.9 = (bf16[8,4,14,768]{3,0,2,1:T(8,128)(2,1)S(1)}, bf16[8,4,14,768]{3,0,2,1:T(8,128)(2,1)S(1)}, u32[]{:S(2)}, u32[]{:S(2)}) collective-permute-start(bf16[8,4,14,768]{3,0,2,1:T(8,128)(2,1)S(1)} %fusion.46), channel_id=1, source_target_pairs={{0,8},{8,0},{1,9},{9,1},{2,10},{10,2},{3,11},{11,3},{4,12},{12,4},... | collective-permute-start | bytes 2064392 | tf_op jit(solution)/shard_map/ppermute | solution.py:91
  308.4 4.4 %copy-start.6 = (s32[64,6]{1,0:T(8,128)S(1)}, s32[64,6]{1,0:T(8,128)}, u32[]{:S(2)}) copy-start(s32[64,6]{1,0:T(8,128)} %copy-done.5) | copy-start | bytes 4612
  308.4 4.5 %copy-start.8 = (bf16[1,2048,32]{1,2,0:T(8,128)(2,1)S(1)}, bf16[1,2048,32]{1,2,0:T(8,128)(2,1)}, u32[]{:S(2)}) copy-start(bf16[1,2048,32]{1,2,0:T(8,128)(2,1)} %param.11) | copy-start | bytes 393220
  308.4 4.5 %copy-start.10 = (bf16[2048,32]{0,1:T(8,128)(2,1)S(1)}, bf16[2048,32]{0,1:T(8,128)(2,1)}, u32[]{:S(2)}) copy-start(bf16[2048,32]{0,1:T(8,128)(2,1)} %copy-done.9) | copy-start | bytes 393220
  308.4 39.5 %all-to-all-start.3 = ((bf16[16,56,1024]{2,1,0:T(8,128)(2,1)}), bf16[16,56,1024]{2,1,0:T(8,128)(2,1)S(1)}, u32[]{:S(2)}, u32[]{:S(2)}) async-start(bf16[16,56,1024]{2,1,0:T(8,128)(2,1)} %copy.96), calls=%async_computation.3 | async-start | bytes 3670016 | tf_op jit(solution)/shard_map/all_to_all | solution.py:99
  351.8 10.2 %all-to-all-start.4 = ((f32[32,1,2]{2,1,0:T(1,128)}), f32[32,1,2]{2,1,0:T(1,128)S(1)}, u32[]{:S(2)}, u32[]{:S(2)}) async-start(f32[32,1,2]{2,1,0:T(1,128)} %broadcast_in_dim.32), calls=%async_computation.4 | async-start | bytes 32768 | tf_op jit(solution)/shard_map/all_to_all | solution.py:144
  354.9 7.7 %collective-permute-start.10 = (bf16[64,1024]{1,0:T(8,128)(2,1)S(1)}, bf16[64,1024]{1,0:T(8,128)(2,1)S(1)}, u32[]{:S(2)}, u32[]{:S(2)}) collective-permute-start(bf16[64,1024]{1,0:T(8,128)(2,1)S(1)} %get-tuple-element.10), channel_id=1, source_target_pairs={{0,16},{16,0},{1,17},{17,1},{2,18},{18,2},{3,19},{19,3},{4,20},{20... | collective-permute-start | bytes 393224 | tf_op jit(solution)/shard_map/ppermute | solution.py:14
  (2 other events, 2.6 us)

commit v4 on v3

--- a/solution.py
+++ b/solution.py
@@ -5,6 +5,7 @@
 
 TOP = 6
 BLOCK = 64
+GROUPS = 2
 
 
 epsilon = 1e-06
@@ -63,54 +64,84 @@
         normed.reshape(normed.shape[0], fsdp_count, chunk),
         preferred_element_type=jnp.float32,
     ).astype(jnp.bfloat16)
-    outgoing = buffer.reshape(peers, local_experts * capacity, chunk)
-    arrived = lax.all_to_all(outgoing, ("fsdp", "expert"), 0, 0, tiled=True)
-    arrived = arrived.reshape(peers, local_experts, capacity, chunk)
     fsdp_index = lax.axis_index("fsdp")
-    gate_part = jnp.einsum("sjcd,jdh->sjch", arrived, gate_w, preferred_element_type=jnp.float32)
-    up_part = jnp.einsum("sjcd,jdh->sjch", arrived, up_w, preferred_element_type=jnp.float32)
-    block_shape = (fsdp_count, expert_devices, local_experts, capacity, hidden_units)
-    gate_blocks = gate_part.reshape(block_shape)
-    up_blocks = up_part.reshape(block_shape)
-    gate_sum = lax.dynamic_index_in_dim(gate_blocks, fsdp_index, 0, keepdims=False)
-    up_sum = lax.dynamic_index_in_dim(up_blocks, fsdp_index, 0, keepdims=False)
-    for shift in range(1, fsdp_count):
-        target = (fsdp_index + shift) % fsdp_count
-        outgoing_pair = jnp.stack(
-            [
-                lax.dynamic_index_in_dim(gate_blocks, target, 0, keepdims=False),
-                lax.dynamic_index_in_dim(up_blocks, target, 0, keepdims=False),
-            ]
+    order = (fsdp_index - jnp.arange(fsdp_count, dtype=jnp.int32)) % fsdp_count
+    combining = jnp.sum(jnp.where(hits, mix_weights[:, :, None], 0.0), axis=1).reshape(
+        -1, expert_devices, local_experts, capacity
+    )
+    slots_in = buffer.reshape(peers, local_experts, capacity, chunk)
+    group_size = local_experts // GROUPS
+    group_slices = [slice(g * group_size, (g + 1) * group_size) for g in range(GROUPS)]
+
+    def dispatch(outgoing):
+        arrived = lax.all_to_all(outgoing, ("fsdp", "expert"), 0, 0, tiled=True)
+        return arrived.reshape(peers, group_size, capacity, chunk)
+
+    def partials(arrived, group_experts):
+        gate_part = jnp.einsum(
+            "sjcd,jdh->sjch", arrived, gate_w[group_experts], preferred_element_type=jnp.float32
+        )
+        up_part = jnp.einsum(
+            "sjcd,jdh->sjch", arrived, up_w[group_experts], preferred_element_type=jnp.float32
+        )
+        block_shape = (fsdp_count, expert_devices, group_size, capacity, hidden_units)
+        return gate_part.reshape(block_shape), up_part.reshape(block_shape)
+
+    def exchange(gate_blocks, up_blocks):
+        gate_sum = lax.dynamic_index_in_dim(gate_blocks, fsdp_index, 0, keepdims=False)
+        up_sum = lax.dynamic_index_in_dim(up_blocks, fsdp_index, 0, keepdims=False)
+        for shift in range(1, fsdp_count):
+            target = (fsdp_index + shift) % fsdp_count
+            outgoing_pair = jnp.stack(
+                [
+                    lax.dynamic_index_in_dim(gate_blocks, target, 0, keepdims=False),
+                    lax.dynamic_index_in_dim(up_blocks, target, 0, keepdims=False),
+                ]
+            ).astype(jnp.bfloat16)
+            got = lax.ppermute(outgoing_pair, "fsdp", ring_pairs(fsdp_count, shift))
+            gate_sum = gate_sum + got[0].astype(jnp.float32)
+            up_sum = up_sum + got[1].astype(jnp.float32)
+        inner_act = (jax.nn.silu(gate_sum) * up_sum).astype(jnp.bfloat16)
+        inner_pieces = [inner_act]
+        for shift in range(1, fsdp_count):
+            inner_pieces.append(lax.ppermute(inner_act, "fsdp", ring_pairs(fsdp_count, shift)))
+        return jnp.take(jnp.stack(inner_pieces), order, axis=0).reshape(
+            peers, group_size, capacity, hidden_units
+        )
+
+    def finish(inner_all, group_experts):
+        produced = jnp.einsum(
+            "sjch,jhd->sjcd", inner_all, down_w[group_experts], preferred_element_type=jnp.float32
         ).astype(jnp.bfloat16)
-        got = lax.ppermute(outgoing_pair, "fsdp", ring_pairs(fsdp_count, shift))
-        gate_sum = gate_sum + got[0].astype(jnp.float32)
-        up_sum = up_sum + got[1].astype(jnp.float32)
-    inner_act = (jax.nn.silu(gate_sum) * up_sum).astype(jnp.bfloat16)
-    inner_pieces = [inner_act]
-    for shift in range(1, fsdp_count):
-        inner_pieces.append(lax.ppermute(inner_act, "fsdp", ring_pairs(fsdp_count, shift)))
-    order = (fsdp_index - jnp.arange(fsdp_count, dtype=jnp.int32)) % fsdp_count
-    inner_all = jnp.take(jnp.stack(inner_pieces), order, axis=0).reshape(
-        peers, local_experts, capacity, hidden_units
-    )
-    produced = jnp.einsum(
-        "sjch,jhd->sjcd", inner_all, down_w, preferred_element_type=jnp.float32
-    ).astype(jnp.bfloat16)
-    returned = lax.all_to_all(
-        produced.reshape(peers, local_experts * capacity, chunk),
-        ("fsdp", "expert"),
-        0,
-        0,
-        tiled=True,
-    )
-    combining = jnp.sum(jnp.where(hits, mix_weights[:, :, None], 0.0), axis=1)
-    branch_sum = jnp.einsum(
-        "rs,fsd->rfd",
-        combining,
-        returned.reshape(fsdp_count, experts_count * capacity, chunk).astype(jnp.float32),
-        precision=lax.Precision.HIGHEST,
-        preferred_element_type=jnp.float32,
-    ).reshape(normed.shape[0], width)
+        returned = lax.all_to_all(
+            produced.reshape(peers, group_size * capacity, chunk),
+            ("fsdp", "expert"),
+            0,
+            0,
+            tiled=True,
+        )
+        return jnp.einsum(
+            "rejc,fejcd->rfd",
+            combining[:, :, group_experts],
+            returned.reshape(fsdp_count, expert_devices, group_size, capacity, chunk).astype(
+                jnp.float32
+            ),
+            precision=lax.Precision.HIGHEST,
+            preferred_element_type=jnp.float32,
+        )
+
+    outgoing = [slots_in[:, g].reshape(peers, group_size * capacity, chunk) for g in group_slices]
+    first_arrived = dispatch(outgoing[0])
+    first_blocks = partials(first_arrived, group_slices[0])
+    second_out, first_blocks = lax.optimization_barrier((outgoing[1], first_blocks))
+    second_arrived = dispatch(second_out)
+    first_inner = exchange(*first_blocks)
+    second_blocks = partials(second_arrived, group_slices[1])
+    first_inner, second_blocks = lax.optimization_barrier((first_inner, second_blocks))
+    branch_sum = finish(first_inner, group_slices[0])
+    second_inner = exchange(*second_blocks)
+    branch_sum = branch_sum + finish(second_inner, group_slices[1])
+    branch_sum = branch_sum.reshape(entering.shape[0], width)
     return (entering.astype(jnp.float32) + branch_sum).astype(jnp.bfloat16)
 
 

time: 364 us -> 389 us (1.069); the launches traced: 363 us -> 381 us
  blocking collectives: 49.6 us -> 0 us
  other arithmetic: 13.8 us -> 44.7 us
  starting transfers between devices: 27.9 us -> 57.4 us
  local copies, waits for them, and re-layouts: 14.3 us -> 42.5 us
  matrix products: 41.4 us -> 29.4 us
  waiting for transfers between devices: 215 us -> 205 us
    all_to_all x1 -> x0, blocking collectives: 49.6 us -> none  [expert_layer(): arrived = lax.all_to_all(outgoing, ('fsdp', 'expert'), 0, 0, tiled=True)]
    all_to_all x3 -> x8, waiting for transfers between devices: 116 us -> 84.9 us  [the longest x4 47 us: dispatch(): arrived = lax.all_to_all(outgoing, ('fsdp', 'expert'), 0, 0, tiled=True)]
    all_to_all x3 -> x8, starting transfers between devices: 16.7 us -> 42.3 us  [the longest x4 22.6 us: finish(): lax.all_to_all(produced.reshape(peers, group_size * capacity, chunk), ('f...]
    select_n x2 -> x4, other arithmetic: 0.71 us -> 24.5 us  [body(): jnp.where(mine, a, b)]
    dot_general x8 -> x16, matrix products: 38.3 us -> 25.1 us  [the longest x4 9.8 us: partials(): jnp.einsum('sjcd,jdh->sjch', arrived, gate_w[group_experts], preferred_el...]
    ppermute x4 -> x8, waiting for transfers between devices: 83.9 us -> 96 us  [the longest x4 72.8 us: exchange(): got = lax.ppermute(outgoing_pair, 'fsdp', ring_pairs(fsdp_count, shift))]
    reshape x2 -> x12, local copies, waits for them, and re-layouts: 4.52 us -> 14.2 us  [the longest x4 6.02 us: finish(): produced.reshape(peers, group_size * capacity, chunk)]
    ppermute x7, waiting for transfers between devices: 8.24 us -> 17.6 us  [other_section(): return lax.ppermute(value, 'section', [(0, 1), (1, 0)])]
  transfers between devices with their start and end apart: 15 -> 24, of which waited for: 10 -> 14; matrix products, arithmetic and copies ran while one was open for 8% -> 20% of each run, Pallas kernels for 0% -> 0%
where the time goes in v4:
time: 389 us; the launch traced here: 381 us
  waiting for transfers between devices  205 us (53%)
  starting transfers between devices  57.4 us (15%)
  other arithmetic  44.7 us (11%)
  local copies, waits for them, and re-layouts  42.5 us (11%)
  matrix products  29.4 us (8%)
    ppermute x4, waiting for transfers between devices, exchange(): got = lax.ppermute(outgoing_pair, 'fsdp', ring_pairs(fsdp_count, shift))  72.8 us
    all_to_all x4, waiting for transfers between devices, dispatch(): arrived = lax.all_to_all(outgoing, ('fsdp', 'expert'), 0, 0, tiled=True)  47 us
    all_to_all x4, waiting for transfers between devices, finish(): lax.all_to_all(produced.reshape(peers, group_size * capacity, chunk), ('f...  38 us
    select_n x4, other arithmetic, body(): jnp.where(mine, a, b)  24.5 us
    ppermute x4, waiting for transfers between devices, exchange(): lax.ppermute(inner_act, 'fsdp', ring_pairs(fsdp_count, shift))  23.2 us
    all_to_all x4, starting transfers between devices, finish(): lax.all_to_all(produced.reshape(peers, group_size * capacity, chunk), ('f...  22.6 us
    all_to_all x4, starting transfers between devices, dispatch(): arrived = lax.all_to_all(outgoing, ('fsdp', 'expert'), 0, 0, tiled=True)  19.8 us
    ppermute x7, waiting for transfers between devices, other_section(): return lax.ppermute(value, 'section', [(0, 1), (1, 0)])  17.6 us
  transfers between devices with their start and end apart: 24, of which 14 were waited for; matrix products, arithmetic and copies ran while one was open for 20% of the time, Pallas kernels for 0%

profile of v4, /device:TPU:0, one launch (start us, length us, event | category | flops | bytes accessed | tf_op | source)
XLA Modules:
  0.0 381.3 jit_solution(2259309389577677867)
XLA Ops:
  3.8 16.6 %collective-permute-done = s32[128,6]{1,0:T(8,128)S(1)} collective-permute-done((s32[128,6]{1,0:T(8,128)S(1)}, s32[128,6]{1,0:T(8,128)S(1)}, u32[]{:S(2)}, u32[]{:S(2)}) %collective-permute-start) | collective-permute-done | bytes 3104 | tf_op jit(solution)/shard_map/ppermute | solution.py:15
  30.9 8.2 %all-to-all-start = ((bf16[16,28,1024]{2,1,0:T(8,128)(2,1)}), bf16[16,28,1024]{2,1,0:T(8,128)(2,1)S(1)}, u32[]{:S(2)}, u32[]{:S(2)}) async-start(bf16[16,28,1024]{2,1,0:T(8,128)(2,1)} %copy.196), calls=%async_computation | async-start | bytes 2097152 | tf_op jit(solution)/shard_map/all_to_all | solution.py:77
  39.7 26.0 %all-to-all-done = bf16[16,28,1024]{2,1,0:T(8,128)(2,1)S(1)} async-done(((bf16[16,28,1024]{2,1,0:T(8,128)(2,1)}), bf16[16,28,1024]{2,1,0:T(8,128)(2,1)S(1)}, u32[]{:S(2)}, u32[]{:S(2)}) %all-to-all-start) | async-done | bytes 917536 | tf_op jit(solution)/shard_map/all_to_all | solution.py:77
  66.3 14.3 %broadcast_select_fusion = (bf16[4,1024,768]{2,1,0:T(8,128)(2,1)}, bf16[4,1024,768]{2,1,0:T(8,128)(2,1)S(1)}, bf16[4,1024,768]{2,1,0:T(8,128)(2,1)S(1)}, bf16[4,1024,768]{2,1,0:T(8,128)(2,1)}) fusion(bf16[4,1024,768]{2,1,0:T(8,128)(2,1)} %collective-permute-done.5, pred[]{:T(512)S(6)} %eq.132, bf16[1,4,1024,768]{3,2,1,0:T(8,128)(2,1)} %param.13, ...), kind=kLoop, calls=%fused_computation.4 | loop fusion | flops 12582912 | bytes 50331648 | tf_op jit(solution)/shard_map/jit(_where)/select_n | solution.py:167
  90.5 3.8 %all-to-all-start.1 = ((bf16[16,28,1024]{2,1,0:T(8,128)(2,1)}), bf16[16,28,1024]{2,1,0:T(8,128)(2,1)S(1)}, u32[]{:S(2)}, u32[]{:S(2)}) async-start(bf16[16,28,1024]{2,1,0:T(8,128)(2,1)} %copy.202), calls=%async_computation.1 | async-start | bytes 2097152 | tf_op jit(solution)/shard_map/all_to_all | solution.py:77
  94.3 17.9 %collective-permute-done.6 = bf16[2,8,2,14,768]{4,1,0,3,2:T(8,128)(2,1)S(1)} collective-permute-done((bf16[2,8,2,14,768]{4,1,0,3,2:T(8,128)(2,1)}, bf16[2,8,2,14,768]{4,1,0,3,2:T(8,128)(2,1)S(1)}, u32[]{:S(2)}, u32[]{:S(2)}) %collective-permute-start.6) | collective-permute-done | bytes 688160 | tf_op jit(solution)/shard_map/ppermute | solution.py:101
  115.9 10.1 %broadcast_select_fusion.2 = (bf16[4,768,1024]{2,1,0:T(8,128)(2,1)}, bf16[4,768,1024]{2,1,0:T(8,128)(2,1)}) fusion(bf16[4,768,1024]{2,1,0:T(8,128)(2,1)} %collective-permute-done.3, pred[]{:T(512)S(6)} %eq.132, bf16[1,4,768,1024]{3,2,1,0:T(8,128)(2,1)} %param.14, pred[]{:T(512)S(6)} %eq.117), kind=kLoop, calls=%fused_computation.6 | loop fusion | flops 6291456 | bytes 25165826 | tf_op jit(solution)/shard_map/jit(_where)/select_n | solution.py:167
  128.7 3.0 fusion.15
  137.4 4.3 %all-to-all-start.2 = ((bf16[16,28,1024]{2,1,0:T(8,128)(2,1)}), bf16[16,28,1024]{2,1,0:T(8,128)(2,1)S(1)}, u32[]{:S(2)}, u32[]{:S(2)}) async-start(bf16[16,28,1024]{2,1,0:T(8,128)(2,1)} %copy.204), calls=%async_computation.2 | async-start | bytes 2097152 | tf_op jit(solution)/shard_map/all_to_all | solution.py:116
  141.7 16.6 %collective-permute-done.8 = bf16[2,8,2,14,768]{4,1,3,2,0:T(8,128)(2,1)S(1)} collective-permute-done((bf16[2,8,2,14,768]{4,1,3,2,0:T(8,128)(2,1)}, bf16[2,8,2,14,768]{4,1,3,2,0:T(8,128)(2,1)S(1)}, u32[]{:S(2)}, u32[]{:S(2)}) %collective-permute-start.8) | collective-permute-done | bytes 688160 | tf_op jit(solution)/shard_map/ppermute | solution.py:101
  161.1 6.3 %collective-permute-done.9 = bf16[8,2,14,768]{3,0,2,1:T(8,128)(2,1)S(1)} collective-permute-done((bf16[8,2,14,768]{3,0,2,1:T(8,128)(2,1)S(1)}, bf16[8,2,14,768]{3,0,2,1:T(8,128)(2,1)S(1)}, u32[]{:S(2)}, u32[]{:S(2)}) %collective-permute-start.9) | collective-permute-done | bytes 344096 | tf_op jit(solution)/shard_map/ppermute | solution.py:107
  172.5 6.2 %all-to-all-start.3 = ((bf16[16,28,1024]{2,1,0:T(8,128)(2,1)}), bf16[16,28,1024]{2,1,0:T(8,128)(2,1)S(1)}, u32[]{:S(2)}, u32[]{:S(2)}) async-start(bf16[16,28,1024]{2,1,0:T(8,128)(2,1)} %copy.212), calls=%async_computation.3 | async-start | bytes 2097152 | tf_op jit(solution)/shard_map/all_to_all | solution.py:116
  182.7 17.1 %all-to-all-done.3 = bf16[16,28,1024]{2,1,0:T(8,128)(2,1)S(1)} async-done(((bf16[16,28,1024]{2,1,0:T(8,128)(2,1)}), bf16[16,28,1024]{2,1,0:T(8,128)(2,1)S(1)}, u32[]{:S(2)}, u32[]{:S(2)}) %all-to-all-start.3) | async-done | bytes 917536 | tf_op jit(solution)/shard_map/all_to_all | solution.py:116
  210.7 3.7 all-to-all-start.4
  217.2 21.0 %all-to-all-done.4 = bf16[16,28,1024]{2,1,0:T(8,128)(2,1)S(1)} async-done(((bf16[16,28,1024]{2,1,0:T(8,128)(2,1)}), bf16[16,28,1024]{2,1,0:T(8,128)(2,1)S(1)}, u32[]{:S(2)}, u32[]{:S(2)}) %all-to-all-start.4) | async-done | bytes 917536 | tf_op jit(solution)/shard_map/all_to_all | solution.py:77
  245.9 4.1 %all-to-all-start.5 = ((bf16[16,28,1024]{2,1,0:T(8,128)(2,1)}), bf16[16,28,1024]{2,1,0:T(8,128)(2,1)S(1)}, u32[]{:S(2)}, u32[]{:S(2)}) async-start(bf16[16,28,1024]{2,1,0:T(8,128)(2,1)} %copy.230), calls=%async_computation.5 | async-start | bytes 2097152 | tf_op jit(solution)/shard_map/all_to_all | solution.py:77
  252.2 24.9 %collective-permute-done.10 = bf16[2,8,2,14,768]{4,1,3,2,0:T(8,128)(2,1)S(1)} collective-permute-done((bf16[2,8,2,14,768]{4,1,3,2,0:T(8,128)(2,1)S(1)}, bf16[2,8,2,14,768]{4,1,3,2,0:T(8,128)(2,1)S(1)}, u32[]{:S(2)}, u32[]{:S(2)}) %collective-permute-start.10) | collective-permute-done | bytes 688160 | tf_op jit(solution)/shard_map/ppermute | solution.py:101
  278.4 8.1 %collective-permute-done.11 = bf16[8,2,14,768]{3,0,2,1:T(8,128)(2,1)S(1)} collective-permute-done((bf16[8,2,14,768]{3,0,2,1:T(8,128)(2,1)S(1)}, bf16[8,2,14,768]{3,0,2,1:T(8,128)(2,1)S(1)}, u32[]{:S(2)}, u32[]{:S(2)}) %collective-permute-start.11) | collective-permute-done | bytes 344096 | tf_op jit(solution)/shard_map/ppermute | solution.py:107
  299.8 5.7 %all-to-all-start.6 = ((bf16[16,28,1024]{2,1,0:T(8,128)(2,1)}), bf16[16,28,1024]{2,1,0:T(8,128)(2,1)S(1)}, u32[]{:S(2)}, u32[]{:S(2)}) async-start(bf16[16,28,1024]{2,1,0:T(8,128)(2,1)} %copy.232), calls=%async_computation.6 | async-start | bytes 2097152 | tf_op jit(solution)/shard_map/all_to_all | solution.py:116
  305.6 13.5 %collective-permute-done.12 = bf16[2,8,2,14,768]{4,1,3,2,0:T(8,128)(2,1)S(1)} collective-permute-done((bf16[2,8,2,14,768]{4,1,3,2,0:T(8,128)(2,1)}, bf16[2,8,2,14,768]{4,1,3,2,0:T(8,128)(2,1)S(1)}, u32[]{:S(2)}, u32[]{:S(2)}) %collective-permute-start.12) | collective-permute-done | bytes 688160 | tf_op jit(solution)/shard_map/ppermute | solution.py:101
  321.9 8.7 %collective-permute-done.13 = bf16[8,2,14,768]{3,0,2,1:T(8,128)(2,1)S(1)} collective-permute-done((bf16[8,2,14,768]{3,0,2,1:T(8,128)(2,1)S(1)}, bf16[8,2,14,768]{3,0,2,1:T(8,128)(2,1)S(1)}, u32[]{:S(2)}, u32[]{:S(2)}) %collective-permute-start.13) | collective-permute-done | bytes 344096 | tf_op jit(solution)/shard_map/ppermute | solution.py:107
  335.6 6.3 %all-to-all-start.7 = ((bf16[16,28,1024]{2,1,0:T(8,128)(2,1)}), bf16[16,28,1024]{2,1,0:T(8,128)(2,1)S(1)}, u32[]{:S(2)}, u32[]{:S(2)}) async-start(bf16[16,28,1024]{2,1,0:T(8,128)(2,1)} %copy.240), calls=%async_computation.7 | async-start | bytes 2097152 | tf_op jit(solution)/shard_map/all_to_all | solution.py:116
  344.2 20.9 %all-to-all-done.7 = bf16[16,28,1024]{2,1,0:T(8,128)(2,1)S(1)} async-done(((bf16[16,28,1024]{2,1,0:T(8,128)(2,1)}), bf16[16,28,1024]{2,1,0:T(8,128)(2,1)S(1)}, u32[]{:S(2)}, u32[]{:S(2)}) %all-to-all-start.7) | async-done | bytes 917536 | tf_op jit(solution)/shard_map/all_to_all | solution.py:116
  372.7 6.7 %all-to-all-done.8 = f32[32,1,2]{2,1,0:T(1,128)S(1)} async-done(((f32[32,1,2]{2,1,0:T(1,128)}), f32[32,1,2]{2,1,0:T(1,128)S(1)}, u32[]{:S(2)}, u32[]{:S(2)}) %all-to-all-start.8) | async-done | bytes 288 | tf_op jit(solution)/shard_map/all_to_all | solution.py:175
  (236 shorter events, 105.3 us)
Async XLA Ops:
  0.7 65.6 %collective-permute-start.5 = (bf16[4,1024,768]{2,1,0:T(8,128)(2,1)}, bf16[4,1024,768]{2,1,0:T(8,128)(2,1)}, u32[]{:S(2)}, u32[]{:S(2)}) collective-permute-start(bf16[4,1024,768]{2,1,0:T(8,128)(2,1)} %bitcast.383), channel_id=1, source_target_pairs={{0,16},{16,0},{1,17},{17,1},{2,18},{18,2},{3,19},{19,3},{4,20},{20... | collective-permute-start | bytes 18874376 | tf_op jit(solution)/shard_map/ppermute | solution.py:15
  1.2 65.0 %collective-permute-start.4 = (bf16[4,1024,768]{2,1,0:T(8,128)(2,1)}, bf16[4,1024,768]{2,1,0:T(8,128)(2,1)}, u32[]{:S(2)}, u32[]{:S(2)}) collective-permute-start(bf16[4,1024,768]{2,1,0:T(8,128)(2,1)} %bitcast.384), channel_id=1, source_target_pairs={{0,16},{16,0},{1,17},{17,1},{2,18},{18,2},{3,19},{19,3},{4,20},{20... | collective-permute-start | bytes 18874376 | tf_op jit(solution)/shard_map/ppermute | solution.py:15
  1.3 22.7 %collective-permute-start.1 = (f32[2048]{0:T(1024)}, f32[2048]{0:T(1024)S(1)}, u32[]{:S(2)}, u32[]{:S(2)}) collective-permute-start(f32[2048]{0:T(1024)} %bitcast.423), channel_id=1, source_target_pairs={{0,16},{16,0},{1,17},{17,1},{2,18},{18,2},{3,19},{19,3},{4,20},{20... | collective-permute-start | bytes 24584 | tf_op jit(solution)/shard_map/ppermute | solution.py:15
  2.5 17.8 %collective-permute-start = (s32[128,6]{1,0:T(8,128)S(1)}, s32[128,6]{1,0:T(8,128)S(1)}, u32[]{:S(2)}, u32[]{:S(2)}) collective-permute-start(s32[128,6]{1,0:T(8,128)S(1)} %bitcast.419), channel_id=1, source_target_pairs={{0,16},{16,0},{1,17},{17,1},{2,18},{18,2},{3,19},{19,3},{4,20},{20... | collective-permute-start | bytes 9224 | tf_op jit(solution)/shard_map/ppermute | solution.py:15
  30.9 34.8 %all-to-all-start = ((bf16[16,28,1024]{2,1,0:T(8,128)(2,1)}), bf16[16,28,1024]{2,1,0:T(8,128)(2,1)S(1)}, u32[]{:S(2)}, u32[]{:S(2)}) async-start(bf16[16,28,1024]{2,1,0:T(8,128)(2,1)} %copy.196), calls=%async_computation | async-start | bytes 2097152 | tf_op jit(solution)/shard_map/all_to_all | solution.py:77
  39.1 76.8 %collective-permute-start.3 = (bf16[4,768,1024]{2,1,0:T(8,128)(2,1)}, bf16[4,768,1024]{2,1,0:T(8,128)(2,1)}, u32[]{:S(2)}, u32[]{:S(2)}) collective-permute-start(bf16[4,768,1024]{2,1,0:T(8,128)(2,1)} %bitcast.378), channel_id=1, source_target_pairs={{0,16},{16,0},{1,17},{17,1},{2,18},{18,2},{3,19},{19,3},{4,20},{20... | collective-permute-start | bytes 18874376 | tf_op jit(solution)/shard_map/ppermute | solution.py:15
  87.5 24.7 %collective-permute-start.6 = (bf16[2,8,2,14,768]{4,1,0,3,2:T(8,128)(2,1)}, bf16[2,8,2,14,768]{4,1,0,3,2:T(8,128)(2,1)S(1)}, u32[]{:S(2)}, u32[]{:S(2)}) collective-permute-start(bf16[2,8,2,14,768]{4,1,0,3,2:T(8,128)(2,1)} %pad_maximum_fusion), channel_id=1, source_target_pairs={{0,8},{8,0},{1,9},{9,1},{2,10},{10,2},{3,11},{11,3},{4,12},{12,4},... | collective-permute-start | bytes 2064392 | tf_op jit(solution)/shard_map/ppermute | solution.py:101
  90.5 37.6 %all-to-all-start.1 = ((bf16[16,28,1024]{2,1,0:T(8,128)(2,1)}), bf16[16,28,1024]{2,1,0:T(8,128)(2,1)S(1)}, u32[]{:S(2)}, u32[]{:S(2)}) async-start(bf16[16,28,1024]{2,1,0:T(8,128)(2,1)} %copy.202), calls=%async_computation.1 | async-start | bytes 2097152 | tf_op jit(solution)/shard_map/all_to_all | solution.py:77
  113.8 12.6 %collective-permute-start.7 = (bf16[8,2,14,768]{3,0,2,1:T(8,128)(2,1)S(1)}, bf16[8,2,14,768]{3,0,2,1:T(8,128)(2,1)S(1)}, u32[]{:S(2)}, u32[]{:S(2)}) collective-permute-start(bf16[8,2,14,768]{3,0,2,1:T(8,128)(2,1)S(1)} %fusion.54), channel_id=1, source_target_pairs={{0,8},{8,0},{1,9},{9,1},{2,10},{10,2},{3,11},{11,3},{4,12},{12,4},... | collective-permute-start | bytes 1032200 | tf_op jit(solution)/shard_map/ppermute | solution.py:107
  134.3 24.0 %collective-permute-start.8 = (bf16[2,8,2,14,768]{4,1,3,2,0:T(8,128)(2,1)}, bf16[2,8,2,14,768]{4,1,3,2,0:T(8,128)(2,1)S(1)}, u32[]{:S(2)}, u32[]{:S(2)}) collective-permute-start(bf16[2,8,2,14,768]{4,1,3,2,0:T(8,128)(2,1)} %pad_maximum_fusion.2), channel_id=1, source_target_pairs={{0,8},{8,0},{1,9},{9,1},{2,10},{10,2},{3,11},{11,3},{4,12},{12,4},... | collective-permute-start | bytes 2064392 | tf_op jit(solution)/shard_map/ppermute | solution.py:101
  137.4 35.1 %all-to-all-start.2 = ((bf16[16,28,1024]{2,1,0:T(8,128)(2,1)}), bf16[16,28,1024]{2,1,0:T(8,128)(2,1)S(1)}, u32[]{:S(2)}, u32[]{:S(2)}) async-start(bf16[16,28,1024]{2,1,0:T(8,128)(2,1)} %copy.204), calls=%async_computation.2 | async-start | bytes 2097152 | tf_op jit(solution)/shard_map/all_to_all | solution.py:116
  159.7 7.8 %collective-permute-start.9 = (bf16[8,2,14,768]{3,0,2,1:T(8,128)(2,1)S(1)}, bf16[8,2,14,768]{3,0,2,1:T(8,128)(2,1)S(1)}, u32[]{:S(2)}, u32[]{:S(2)}) collective-permute-start(bf16[8,2,14,768]{3,0,2,1:T(8,128)(2,1)S(1)} %fusion.50), channel_id=1, source_target_pairs={{0,8},{8,0},{1,9},{9,1},{2,10},{10,2},{3,11},{11,3},{4,12},{12,4},... | collective-permute-start | bytes 1032200 | tf_op jit(solution)/shard_map/ppermute | solution.py:107
  172.5 27.3 %all-to-all-start.3 = ((bf16[16,28,1024]{2,1,0:T(8,128)(2,1)}), bf16[16,28,1024]{2,1,0:T(8,128)(2,1)S(1)}, u32[]{:S(2)}, u32[]{:S(2)}) async-start(bf16[16,28,1024]{2,1,0:T(8,128)(2,1)} %copy.212), calls=%async_computation.3 | async-start | bytes 2097152 | tf_op jit(solution)/shard_map/all_to_all | solution.py:116
  178.7 1.4 collective-permute-start.2
  210.7 27.5 %all-to-all-start.4 = ((bf16[16,28,1024]{2,1,0:T(8,128)(2,1)}), bf16[16,28,1024]{2,1,0:T(8,128)(2,1)S(1)}, u32[]{:S(2)}, u32[]{:S(2)}) async-start(bf16[16,28,1024]{2,1,0:T(8,128)(2,1)} %copy.223), calls=%async_computation.4 | async-start | bytes 2097152 | tf_op jit(solution)/shard_map/all_to_all | solution.py:77
  245.9 44.4 %all-to-all-start.5 = ((bf16[16,28,1024]{2,1,0:T(8,128)(2,1)}), bf16[16,28,1024]{2,1,0:T(8,128)(2,1)S(1)}, u32[]{:S(2)}, u32[]{:S(2)}) async-start(bf16[16,28,1024]{2,1,0:T(8,128)(2,1)} %copy.230), calls=%async_computation.5 | async-start | bytes 2097152 | tf_op jit(solution)/shard_map/all_to_all | solution.py:77
  250.1 27.0 %collective-permute-start.10 = (bf16[2,8,2,14,768]{4,1,3,2,0:T(8,128)(2,1)S(1)}, bf16[2,8,2,14,768]{4,1,3,2,0:T(8,128)(2,1)S(1)}, u32[]{:S(2)}, u32[]{:S(2)}) collective-permute-start(bf16[2,8,2,14,768]{4,1,3,2,0:T(8,128)(2,1)S(1)} %pad_maximum_fusion.4), channel_id=1, source_target_pairs={{0,8},{8,0},{1,9},{9,1},{2,10},{10,2},{3,11},{11,3},{4,12},{12,4},... | collective-permute-start | bytes 2064392 | tf_op jit(solution)/shard_map/ppermute | solution.py:101
  277.3 9.2 %collective-permute-start.11 = (bf16[8,2,14,768]{3,0,2,1:T(8,128)(2,1)S(1)}, bf16[8,2,14,768]{3,0,2,1:T(8,128)(2,1)S(1)}, u32[]{:S(2)}, u32[]{:S(2)}) collective-permute-start(bf16[8,2,14,768]{3,0,2,1:T(8,128)(2,1)S(1)} %fusion.45), channel_id=1, source_target_pairs={{0,8},{8,0},{1,9},{9,1},{2,10},{10,2},{3,11},{11,3},{4,12},{12,4},... | collective-permute-start | bytes 1032200 | tf_op jit(solution)/shard_map/ppermute | solution.py:107
  296.2 22.8 %collective-permute-start.12 = (bf16[2,8,2,14,768]{4,1,3,2,0:T(8,128)(2,1)}, bf16[2,8,2,14,768]{4,1,3,2,0:T(8,128)(2,1)S(1)}, u32[]{:S(2)}, u32[]{:S(2)}) collective-permute-start(bf16[2,8,2,14,768]{4,1,3,2,0:T(8,128)(2,1)} %pad_maximum_fusion.6), channel_id=1, source_target_pairs={{0,8},{8,0},{1,9},{9,1},{2,10},{10,2},{3,11},{11,3},{4,12},{12,4},... | collective-permute-start | bytes 2064392 | tf_op jit(solution)/shard_map/ppermute | solution.py:101
  299.8 35.8 %all-to-all-start.6 = ((bf16[16,28,1024]{2,1,0:T(8,128)(2,1)}), bf16[16,28,1024]{2,1,0:T(8,128)(2,1)S(1)}, u32[]{:S(2)}, u32[]{:S(2)}) async-start(bf16[16,28,1024]{2,1,0:T(8,128)(2,1)} %copy.232), calls=%async_computation.6 | async-start | bytes 2097152 | tf_op jit(solution)/shard_map/all_to_all | solution.py:116
  320.4 10.2 %collective-permute-start.13 = (bf16[8,2,14,768]{3,0,2,1:T(8,128)(2,1)S(1)}, bf16[8,2,14,768]{3,0,2,1:T(8,128)(2,1)S(1)}, u32[]{:S(2)}, u32[]{:S(2)}) collective-permute-start(bf16[8,2,14,768]{3,0,2,1:T(8,128)(2,1)S(1)} %fusion.41), channel_id=1, source_target_pairs={{0,8},{8,0},{1,9},{9,1},{2,10},{10,2},{3,11},{11,3},{4,12},{12,4},... | collective-permute-start | bytes 1032200 | tf_op jit(solution)/shard_map/ppermute | solution.py:107
  335.6 29.6 %all-to-all-start.7 = ((bf16[16,28,1024]{2,1,0:T(8,128)(2,1)}), bf16[16,28,1024]{2,1,0:T(8,128)(2,1)S(1)}, u32[]{:S(2)}, u32[]{:S(2)}) async-start(bf16[16,28,1024]{2,1,0:T(8,128)(2,1)} %copy.240), calls=%async_computation.7 | async-start | bytes 2097152 | tf_op jit(solution)/shard_map/all_to_all | solution.py:116
  369.5 9.9 %all-to-all-start.8 = ((f32[32,1,2]{2,1,0:T(1,128)}), f32[32,1,2]{2,1,0:T(1,128)S(1)}, u32[]{:S(2)}, u32[]{:S(2)}) async-start(f32[32,1,2]{2,1,0:T(1,128)} %broadcast_in_dim.32), calls=%async_computation.8 | async-start | bytes 32768 | tf_op jit(solution)/shard_map/all_to_all | solution.py:175
  372.4 7.7 %collective-permute-start.14 = (bf16[64,1024]{1,0:T(8,128)(2,1)S(1)}, bf16[64,1024]{1,0:T(8,128)(2,1)S(1)}, u32[]{:S(2)}, u32[]{:S(2)}) collective-permute-start(bf16[64,1024]{1,0:T(8,128)(2,1)S(1)} %get-tuple-element.47), channel_id=1, source_target_pairs={{0,16},{16,0},{1,17},{17,1},{2,18},{18,2},{3,19},{19,3},{4,20},{20... | collective-permute-start | bytes 393224 | tf_op jit(solution)/shard_map/ppermute | solution.py:15
  (38 other events, 300.8 us)

commit v5 on v4

--- a/solution.py
+++ b/solution.py
@@ -5,7 +5,7 @@
 
 TOP = 6
 BLOCK = 64
-GROUPS = 2
+GROUPS = 4
 
 
 epsilon = 1e-06
@@ -131,16 +131,18 @@
         )
 
     outgoing = [slots_in[:, g].reshape(peers, group_size * capacity, chunk) for g in group_slices]
-    first_arrived = dispatch(outgoing[0])
-    first_blocks = partials(first_arrived, group_slices[0])
-    second_out, first_blocks = lax.optimization_barrier((outgoing[1], first_blocks))
-    second_arrived = dispatch(second_out)
-    first_inner = exchange(*first_blocks)
-    second_blocks = partials(second_arrived, group_slices[1])
-    first_inner, second_blocks = lax.optimization_barrier((first_inner, second_blocks))
-    branch_sum = finish(first_inner, group_slices[0])
-    second_inner = exchange(*second_blocks)
-    branch_sum = branch_sum + finish(second_inner, group_slices[1])
+    blocks = partials(dispatch(outgoing[0]), group_slices[0])
+    branch_sum = None
+    for group in range(1, GROUPS):
+        next_out, blocks = lax.optimization_barrier((outgoing[group], blocks))
+        next_arrived = dispatch(next_out)
+        inner_all = exchange(*blocks)
+        blocks = partials(next_arrived, group_slices[group])
+        inner_all, blocks = lax.optimization_barrier((inner_all, blocks))
+        finished = finish(inner_all, group_slices[group - 1])
+        branch_sum = finished if branch_sum is None else branch_sum + finished
+    finished = finish(exchange(*blocks), group_slices[GROUPS - 1])
+    branch_sum = finished if branch_sum is None else branch_sum + finished
     branch_sum = branch_sum.reshape(entering.shape[0], width)
     return (entering.astype(jnp.float32) + branch_sum).astype(jnp.bfloat16)
 
@@ -153,8 +155,9 @@
     experts_count = router.shape[2]
     block_capacity = (7 * BLOCK * TOP + 6 * experts_count - 1) // (6 * experts_count)
     capacity = block_capacity * (piece // BLOCK)
-    own_weights = (w_gate[0], w_up[0], w_down[0])
-    other_weights = tuple(other_section(w) for w in own_weights)
+    layer_weights = tuple(
+        lax.all_gather(w[0], "section", axis=0, tiled=False) for w in (w_gate, w_up, w_down)
+    )
     own_small = (norm_gain[0], router[0], routes[0])
     other_small = tuple(other_section(v) for v in own_small)
     hidden = lax.dynamic_slice_in_dim(tokens, section_index * piece, piece, 0)
@@ -164,7 +167,7 @@
         gain_row, router_weight, route_all = [
             jnp.where(mine, a, b) for a, b in zip(own_small, other_small)
         ]
-        weights = tuple(jnp.where(mine, a, b) for a, b in zip(own_weights, other_weights))
+        weights = tuple(w[layer] for w in layer_weights)
         route_rows = lax.dynamic_slice_in_dim(route_all, section_index * piece, piece, 0)
         hidden = expert_layer(hidden, route_rows, gain_row, router_weight, weights, capacity)
         values = hidden.astype(jnp.float32)

time: 389 us -> 414 us (1.064); the launches traced: 381 us -> 411 us
  starting transfers between devices: 57.4 us -> 102 us
  waiting for transfers between devices: 205 us -> 167 us
  matrix products: 29.4 us -> 60.1 us
  other arithmetic: 44.7 us -> 22.3 us
  blocking collectives: 0 us -> 17.4 us
  local copies, waits for them, and re-layouts: 42.5 us -> 27.4 us
  between operations: 2.03 us -> 14.9 us
    ppermute x4 -> x8, waiting for transfers between devices: 72.8 us -> 32.3 us  [exchange(): got = lax.ppermute(outgoing_pair, 'fsdp', ring_pairs(fsdp_count, shift))]
    all_to_all x4 -> x7, waiting for transfers between devices: 47 us -> 20.1 us  [dispatch(): arrived = lax.all_to_all(outgoing, ('fsdp', 'expert'), 0, 0, tiled=True)]
    select_n x4 -> x2, other arithmetic: 24.5 us -> 0.01 us  [body(): jnp.where(mine, a, b)]
    all_to_all x4 -> x8, waiting for transfers between devices: 38 us -> 59.2 us  [finish(): lax.all_to_all(produced.reshape(peers, group_size * capacity, chunk), ('f...]
    all_to_all x0 -> x1, blocking collectives: none -> 17.4 us  [dispatch(): arrived = lax.all_to_all(outgoing, ('fsdp', 'expert'), 0, 0, tiled=True)]
    all_gather x0 -> x3, waiting for transfers between devices: none -> 17.1 us  [body(): lax.all_gather(w[0], 'section', axis=0, tiled=False)]
    ppermute x7 -> x4, waiting for transfers between devices: 17.6 us -> 1.06 us  [other_section(): return lax.ppermute(value, 'section', [(0, 1), (1, 0)])]
    dot_general x4 -> x8, matrix products: 3.56 us -> 17.3 us  [partials(): jnp.einsum('sjcd,jdh->sjch', arrived, up_w[group_experts], preferred_elem...]
  transfers between devices with their start and end apart: 24 -> 39, of which waited for: 14 -> 26; matrix products, arithmetic and copies ran while one was open for 20% -> 21% of each run, Pallas kernels for 0% -> 0%
where the time goes in v5:
time: 414 us; the launch traced here: 411 us
  waiting for transfers between devices  167 us (40%)
  starting transfers between devices  102 us (25%)
  matrix products  60.1 us (15%)
  local copies, waits for them, and re-layouts  27.4 us (7%)
  other arithmetic  22.3 us (5%)
  blocking collectives  17.4 us (4%)
  between operations  14.9 us (4%)
    all_to_all x8, waiting for transfers between devices, finish(): lax.all_to_all(produced.reshape(peers, group_size * capacity, chunk), ('f...  59.2 us
    all_to_all x8, starting transfers between devices, finish(): lax.all_to_all(produced.reshape(peers, group_size * capacity, chunk), ('f...  35.4 us
    all_to_all x7, starting transfers between devices, dispatch(): arrived = lax.all_to_all(outgoing, ('fsdp', 'expert'), 0, 0, tiled=True)  32.6 us
    ppermute x8, waiting for transfers between devices, exchange(): got = lax.ppermute(outgoing_pair, 'fsdp', ring_pairs(fsdp_count, shift))  32.3 us
    ppermute x8, waiting for transfers between devices, exchange(): lax.ppermute(inner_act, 'fsdp', ring_pairs(fsdp_count, shift))  28.1 us
    all_to_all x7, waiting for transfers between devices, dispatch(): arrived = lax.all_to_all(outgoing, ('fsdp', 'expert'), 0, 0, tiled=True)  20.1 us
    all_to_all x1, blocking collectives, dispatch(): arrived = lax.all_to_all(outgoing, ('fsdp', 'expert'), 0, 0, tiled=True)  17.4 us
    dot_general x8, matrix products, partials(): jnp.einsum('sjcd,jdh->sjch', arrived, up_w[group_experts], preferred_elem...  17.3 us
  transfers between devices with their start and end apart: 39, of which 26 were waited for; matrix products, arithmetic and copies ran while one was open for 21% of the time, Pallas kernels for 0%

profile of v5, /device:TPU:0, one launch (start us, length us, event | category | flops | bytes accessed | tf_op | source)
XLA Modules:
  0.0 411.1 jit_solution(758172686032024537)
XLA Ops:
  21.3 8.1 %all-to-all-start = ((bf16[16,14,1024]{2,1,0:T(8,128)(2,1)}), bf16[16,14,1024]{2,1,0:T(8,128)(2,1)S(1)}, u32[]{:S(2)}, u32[]{:S(2)}) async-start(bf16[16,14,1024]{2,1,0:T(8,128)(2,1)} %get-tuple-element.90), calls=%async_computation | async-start | bytes 1048576 | tf_op jit(solution)/shard_map/all_to_all | solution.py:77
  29.4 15.5 %all-to-all-done = bf16[16,14,1024]{2,1,0:T(8,128)(2,1)S(1)} async-done(((bf16[16,14,1024]{2,1,0:T(8,128)(2,1)}), bf16[16,14,1024]{2,1,0:T(8,128)(2,1)S(1)}, u32[]{:S(2)}, u32[]{:S(2)}) %all-to-all-start) | async-done | bytes 458784 | tf_op jit(solution)/shard_map/all_to_all | solution.py:77
  47.3 17.1 %all-gather.4.cloned.1.call-done = bf16[2,4,1024,768]{3,2,1,0:T(8,128)(2,1)} async-done(((bf16[1,4,1024,768]{3,2,1,0:T(8,128)(2,1)}), bf16[2,4,1024,768]{3,2,1,0:T(8,128)(2,1)}) %all-gather.4.cloned.1.call-update) | async-done | bytes 12582928 | tf_op jit(solution)/shard_map/all_gather | solution.py:159
  69.2 5.6 %all-to-all-start.1 = ((bf16[16,14,1024]{2,1,0:T(8,128)(2,1)}), bf16[16,14,1024]{2,1,0:T(8,128)(2,1)S(1)}, u32[]{:S(2)}, u32[]{:S(2)}) async-start(bf16[16,14,1024]{2,1,0:T(8,128)(2,1)} %get-tuple-element.41), calls=%async_computation.1 | async-start | bytes 1048576 | tf_op jit(solution)/shard_map/all_to_all | solution.py:77
  75.6 4.5 %collective-permute-done.3 = bf16[2,8,1,14,768]{4,1,0,3,2:T(8,128)(2,1)S(1)} collective-permute-done((bf16[2,8,1,14,768]{4,1,0,3,2:T(8,128)(2,1)}, bf16[2,8,1,14,768]{4,1,0,3,2:T(8,128)(2,1)S(1)}, u32[]{:S(2)}, u32[]{:S(2)}) %collective-permute-start.3) | collective-permute-done | bytes 344096 | tf_op jit(solution)/shard_map/ppermute | solution.py:101
  102.1 4.3 %collective-permute-done.5 = bf16[2,8,1,14,768]{4,1,3,2,0:T(8,128)(2,1)S(1)} collective-permute-done((bf16[2,8,1,14,768]{4,1,3,2,0:T(8,128)(2,1)}, bf16[2,8,1,14,768]{4,1,3,2,0:T(8,128)(2,1)S(1)}, u32[]{:S(2)}, u32[]{:S(2)}) %collective-permute-start.5) | collective-permute-done | bytes 344096 | tf_op jit(solution)/shard_map/ppermute | solution.py:101
  134.0 6.1 %collective-permute-done.7 = bf16[2,8,1,14,768]{4,1,3,2,0:T(8,128)(2,1)S(1)} collective-permute-done((bf16[2,8,1,14,768]{4,1,3,2,0:T(8,128)(2,1)}, bf16[2,8,1,14,768]{4,1,3,2,0:T(8,128)(2,1)S(1)}, u32[]{:S(2)}, u32[]{:S(2)}) %collective-permute-start.7) | collective-permute-done | bytes 344096 | tf_op jit(solution)/shard_map/ppermute | solution.py:101
  141.7 6.0 %all-to-all-start.2 = ((bf16[16,14,1024]{2,1,0:T(8,128)(2,1)}), bf16[16,14,1024]{2,1,0:T(8,128)(2,1)S(1)}, u32[]{:S(2)}, u32[]{:S(2)}) async-start(bf16[16,14,1024]{2,1,0:T(8,128)(2,1)} %copy.323), calls=%async_computation.2 | async-start | bytes 1048576 | tf_op jit(solution)/shard_map/all_to_all | solution.py:116
  153.8 8.2 %all-to-all-done.2 = bf16[16,14,1024]{2,1,0:T(8,128)(2,1)S(1)} async-done(((bf16[16,14,1024]{2,1,0:T(8,128)(2,1)}), bf16[16,14,1024]{2,1,0:T(8,128)(2,1)S(1)}, u32[]{:S(2)}, u32[]{:S(2)}) %all-to-all-start.2) | async-done | bytes 458784 | tf_op jit(solution)/shard_map/all_to_all | solution.py:116
  172.1 7.7 %all-to-all-done.4 = bf16[16,14,1024]{2,1,0:T(8,128)(2,1)S(1)} async-done(((bf16[16,14,1024]{2,1,0:T(8,128)(2,1)}), bf16[16,14,1024]{2,1,0:T(8,128)(2,1)S(1)}, u32[]{:S(2)}, u32[]{:S(2)}) %all-to-all-start.4) | async-done | bytes 458784 | tf_op jit(solution)/shard_map/all_to_all | solution.py:116
  187.6 5.7 %collective-permute-done.10 = bf16[8,1,14,768]{3,0,2,1:T(8,128)(2,1)S(1)} collective-permute-done((bf16[8,1,14,768]{3,0,2,1:T(8,128)(2,1)S(1)}, bf16[8,1,14,768]{3,0,2,1:T(8,128)(2,1)S(1)}, u32[]{:S(2)}, u32[]{:S(2)}) %collective-permute-start.10) | collective-permute-done | bytes 172064 | tf_op jit(solution)/shard_map/ppermute | solution.py:107
  197.4 5.6 %all-to-all-start.7 = ((bf16[16,14,1024]{2,1,0:T(8,128)(2,1)}), bf16[16,14,1024]{2,1,0:T(8,128)(2,1)S(1)}, u32[]{:S(2)}, u32[]{:S(2)}) async-start(bf16[16,14,1024]{2,1,0:T(8,128)(2,1)} %copy.348), calls=%async_computation.7 | async-start | bytes 1048576 | tf_op jit(solution)/shard_map/all_to_all | solution.py:116
  204.7 12.1 %all-to-all-done.7 = bf16[16,14,1024]{2,1,0:T(8,128)(2,1)S(1)} async-done(((bf16[16,14,1024]{2,1,0:T(8,128)(2,1)}), bf16[16,14,1024]{2,1,0:T(8,128)(2,1)S(1)}, u32[]{:S(2)}, u32[]{:S(2)}) %all-to-all-start.7) | async-done | bytes 458784 | tf_op jit(solution)/shard_map/all_to_all | solution.py:116
  223.8 17.4 %all_to_all.86 = bf16[16,14,1024]{2,1,0:T(8,128)(2,1)S(1)} all-to-all(bf16[16,14,1024]{2,1,0:T(8,128)(2,1)S(1)} %get-tuple-element.86), channel_id=1, replica_groups=mesh['section'=2,'fsdp'=2,'expert'=8] {'fsdp','expert'}, dimensions={0} | all-to-all | bytes 917504 | tf_op jit(solution)/shard_map/all_to_all | solution.py:77
  251.3 7.5 %collective-permute-done.11 = bf16[2,8,1,14,768]{4,1,3,2,0:T(8,128)(2,1)S(1)} collective-permute-done((bf16[2,8,1,14,768]{4,1,3,2,0:T(8,128)(2,1)}, bf16[2,8,1,14,768]{4,1,3,2,0:T(8,128)(2,1)S(1)}, u32[]{:S(2)}, u32[]{:S(2)}) %collective-permute-start.11) | collective-permute-done | bytes 344096 | tf_op jit(solution)/shard_map/ppermute | solution.py:101
  279.6 4.6 %collective-permute-done.13 = bf16[2,8,1,14,768]{4,1,3,2,0:T(8,128)(2,1)S(1)} collective-permute-done((bf16[2,8,1,14,768]{4,1,3,2,0:T(8,128)(2,1)S(1)}, bf16[2,8,1,14,768]{4,1,3,2,0:T(8,128)(2,1)S(1)}, u32[]{:S(2)}, u32[]{:S(2)}) %collective-permute-start.13) | collective-permute-done | bytes 344096 | tf_op jit(solution)/shard_map/ppermute | solution.py:101
  286.9 4.2 %collective-permute-done.14 = bf16[8,1,14,768]{3,0,2,1:T(8,128)(2,1)S(1)} collective-permute-done((bf16[8,1,14,768]{3,0,2,1:T(8,128)(2,1)S(1)}, bf16[8,1,14,768]{3,0,2,1:T(8,128)(2,1)S(1)}, u32[]{:S(2)}, u32[]{:S(2)}) %collective-permute-start.14) | collective-permute-done | bytes 172064 | tf_op jit(solution)/shard_map/ppermute | solution.py:107
  308.6 5.2 %collective-permute-done.15 = bf16[2,8,1,14,768]{4,1,3,2,0:T(8,128)(2,1)S(1)} collective-permute-done((bf16[2,8,1,14,768]{4,1,3,2,0:T(8,128)(2,1)S(1)}, bf16[2,8,1,14,768]{4,1,3,2,0:T(8,128)(2,1)S(1)}, u32[]{:S(2)}, u32[]{:S(2)}) %collective-permute-start.15) | collective-permute-done | bytes 344096 | tf_op jit(solution)/shard_map/ppermute | solution.py:101
  315.5 6.0 %all-to-all-start.10 = ((bf16[16,14,1024]{2,1,0:T(8,128)(2,1)}), bf16[16,14,1024]{2,1,0:T(8,128)(2,1)S(1)}, u32[]{:S(2)}, u32[]{:S(2)}) async-start(bf16[16,14,1024]{2,1,0:T(8,128)(2,1)} %copy.365), calls=%async_computation.10 | async-start | bytes 1048576 | tf_op jit(solution)/shard_map/all_to_all | solution.py:116
  327.6 9.7 %all-to-all-done.10 = bf16[16,14,1024]{2,1,0:T(8,128)(2,1)S(1)} async-done(((bf16[16,14,1024]{2,1,0:T(8,128)(2,1)}), bf16[16,14,1024]{2,1,0:T(8,128)(2,1)S(1)}, u32[]{:S(2)}, u32[]{:S(2)}) %all-to-all-start.10) | async-done | bytes 458784 | tf_op jit(solution)/shard_map/all_to_all | solution.py:116
  347.3 8.7 %all-to-all-done.12 = bf16[16,14,1024]{2,1,0:T(8,128)(2,1)S(1)} async-done(((bf16[16,14,1024]{2,1,0:T(8,128)(2,1)}), bf16[16,14,1024]{2,1,0:T(8,128)(2,1)S(1)}, u32[]{:S(2)}, u32[]{:S(2)}) %all-to-all-start.12) | async-done | bytes 458784 | tf_op jit(solution)/shard_map/all_to_all | solution.py:116
  361.9 6.6 %collective-permute-done.18 = bf16[8,1,14,768]{3,0,2,1:T(8,128)(2,1)S(1)} collective-permute-done((bf16[8,1,14,768]{3,0,2,1:T(8,128)(2,1)S(1)}, bf16[8,1,14,768]{3,0,2,1:T(8,128)(2,1)S(1)}, u32[]{:S(2)}, u32[]{:S(2)}) %collective-permute-start.18) | collective-permute-done | bytes 172064 | tf_op jit(solution)/shard_map/ppermute | solution.py:107
  381.1 9.0 %all-to-all-done.15 = bf16[16,14,1024]{2,1,0:T(8,128)(2,1)S(1)} async-done(((bf16[16,14,1024]{2,1,0:T(8,128)(2,1)}), bf16[16,14,1024]{2,1,0:T(8,128)(2,1)S(1)}, u32[]{:S(2)}, u32[]{:S(2)}) %all-to-all-start.15) | async-done | bytes 458784 | tf_op jit(solution)/shard_map/all_to_all | solution.py:116
  396.4 6.7 %all-to-all-done.16 = f32[32,1,2]{2,1,0:T(1,128)S(1)} async-done(((f32[32,1,2]{2,1,0:T(1,128)}), f32[32,1,2]{2,1,0:T(1,128)S(1)}, u32[]{:S(2)}, u32[]{:S(2)}) %all-to-all-start.16) | async-done | bytes 288 | tf_op jit(solution)/shard_map/all_to_all | solution.py:178
  (267 shorter events, 204.1 us)
Async XLA Ops:
  7.2 37.7 %all-gather.6.cloned.1.call-start = ((), (), s32[]{:S(2)}) async-start(), calls=%async_computation.18 | async-start | bytes 18874368 | tf_op jit(solution)/shard_map/all_gather | solution.py:159
  7.9 56.6 %all-gather.4.cloned.1.call-start = ((), (), s32[]{:S(2)}) async-start(), calls=%async_computation.17 | async-start | bytes 18874368 | tf_op jit(solution)/shard_map/all_gather | solution.py:159
  8.7 119.1 %all-gather.8.cloned.1.call-start = ((), (), s32[]{:S(2)}) async-start(), calls=%async_computation.19 | async-start | bytes 18874368 | tf_op jit(solution)/shard_map/all_gather | solution.py:159
  21.3 23.6 %all-to-all-start = ((bf16[16,14,1024]{2,1,0:T(8,128)(2,1)}), bf16[16,14,1024]{2,1,0:T(8,128)(2,1)S(1)}, u32[]{:S(2)}, u32[]{:S(2)}) async-start(bf16[16,14,1024]{2,1,0:T(8,128)(2,1)} %get-tuple-element.90), calls=%async_computation | async-start | bytes 1048576 | tf_op jit(solution)/shard_map/all_to_all | solution.py:77
  67.4 12.7 %collective-permute-start.3 = (bf16[2,8,1,14,768]{4,1,0,3,2:T(8,128)(2,1)}, bf16[2,8,1,14,768]{4,1,0,3,2:T(8,128)(2,1)S(1)}, u32[]{:S(2)}, u32[]{:S(2)}) collective-permute-start(bf16[2,8,1,14,768]{4,1,0,3,2:T(8,128)(2,1)} %pad_maximum_fusion), channel_id=1, source_target_pairs={{0,8},{8,0},{1,9},{9,1},{2,10},{10,2},{3,11},{11,3},{4,12},{12,4},... | collective-permute-start | bytes 1032200 | tf_op jit(solution)/shard_map/ppermute | solution.py:101
  69.1 28.0 %collective-permute-start.2 = (bf16[2048,32]{0,1:T(8,128)(2,1)}, bf16[2048,32]{0,1:T(8,128)(2,1)}, u32[]{:S(2)}, u32[]{:S(2)}) collective-permute-start(bf16[2048,32]{0,1:T(8,128)(2,1)} %bitcast.757), channel_id=1, source_target_pairs={{0,16},{16,0},{1,17},{17,1},{2,18},{18,2},{3,19},{19,3},{4,20},{20... | collective-permute-start | bytes 393224 | tf_op jit(solution)/shard_map/ppermute | solution.py:15
  69.2 21.2 %all-to-all-start.1 = ((bf16[16,14,1024]{2,1,0:T(8,128)(2,1)}), bf16[16,14,1024]{2,1,0:T(8,128)(2,1)S(1)}, u32[]{:S(2)}, u32[]{:S(2)}) async-start(bf16[16,14,1024]{2,1,0:T(8,128)(2,1)} %get-tuple-element.41), calls=%async_computation.1 | async-start | bytes 1048576 | tf_op jit(solution)/shard_map/all_to_all | solution.py:77
  98.0 19.3 %all-to-all-start.3 = ((bf16[16,14,1024]{2,1,0:T(8,128)(2,1)}), bf16[16,14,1024]{2,1,0:T(8,128)(2,1)S(1)}, u32[]{:S(2)}, u32[]{:S(2)}) async-start(bf16[16,14,1024]{2,1,0:T(8,128)(2,1)} %get-tuple-element.47), calls=%async_computation.3 | async-start | bytes 1048576 | tf_op jit(solution)/shard_map/all_to_all | solution.py:77
  121.5 19.5 %all-to-all-start.5 = ((bf16[16,14,1024]{2,1,0:T(8,128)(2,1)}), bf16[16,14,1024]{2,1,0:T(8,128)(2,1)S(1)}, u32[]{:S(2)}, u32[]{:S(2)}) async-start(bf16[16,14,1024]{2,1,0:T(8,128)(2,1)} %get-tuple-element.53), calls=%async_computation.5 | async-start | bytes 1048576 | tf_op jit(solution)/shard_map/all_to_all | solution.py:77
  125.9 14.3 %collective-permute-start.7 = (bf16[2,8,1,14,768]{4,1,3,2,0:T(8,128)(2,1)}, bf16[2,8,1,14,768]{4,1,3,2,0:T(8,128)(2,1)S(1)}, u32[]{:S(2)}, u32[]{:S(2)}) collective-permute-start(bf16[2,8,1,14,768]{4,1,3,2,0:T(8,128)(2,1)} %pad_maximum_fusion.2), channel_id=1, source_target_pairs={{0,8},{8,0},{1,9},{9,1},{2,10},{10,2},{3,11},{11,3},{4,12},{12,4},... | collective-permute-start | bytes 1032200 | tf_op jit(solution)/shard_map/ppermute | solution.py:101
  141.7 20.3 %all-to-all-start.2 = ((bf16[16,14,1024]{2,1,0:T(8,128)(2,1)}), bf16[16,14,1024]{2,1,0:T(8,128)(2,1)S(1)}, u32[]{:S(2)}, u32[]{:S(2)}) async-start(bf16[16,14,1024]{2,1,0:T(8,128)(2,1)} %copy.323), calls=%async_computation.2 | async-start | bytes 1048576 | tf_op jit(solution)/shard_map/all_to_all | solution.py:116
  162.1 17.8 %all-to-all-start.4 = ((bf16[16,14,1024]{2,1,0:T(8,128)(2,1)}), bf16[16,14,1024]{2,1,0:T(8,128)(2,1)S(1)}, u32[]{:S(2)}, u32[]{:S(2)}) async-start(bf16[16,14,1024]{2,1,0:T(8,128)(2,1)} %copy.332), calls=%async_computation.4 | async-start | bytes 1048576 | tf_op jit(solution)/shard_map/all_to_all | solution.py:116
  166.5 16.9 %collective-permute-start.9 = (bf16[2,8,1,14,768]{4,1,3,2,0:T(8,128)(2,1)}, bf16[2,8,1,14,768]{4,1,3,2,0:T(8,128)(2,1)S(1)}, u32[]{:S(2)}, u32[]{:S(2)}) collective-permute-start(bf16[2,8,1,14,768]{4,1,3,2,0:T(8,128)(2,1)} %pad_maximum_fusion.3), channel_id=1, source_target_pairs={{0,8},{8,0},{1,9},{9,1},{2,10},{10,2},{3,11},{11,3},{4,12},{12,4},... | collective-permute-start | bytes 1032200 | tf_op jit(solution)/shard_map/ppermute | solution.py:101
  179.8 17.6 %all-to-all-start.6 = ((bf16[16,14,1024]{2,1,0:T(8,128)(2,1)}), bf16[16,14,1024]{2,1,0:T(8,128)(2,1)S(1)}, u32[]{:S(2)}, u32[]{:S(2)}) async-start(bf16[16,14,1024]{2,1,0:T(8,128)(2,1)} %copy.341), calls=%async_computation.6 | async-start | bytes 1048576 | tf_op jit(solution)/shard_map/all_to_all | solution.py:116
  197.4 19.3 %all-to-all-start.7 = ((bf16[16,14,1024]{2,1,0:T(8,128)(2,1)}), bf16[16,14,1024]{2,1,0:T(8,128)(2,1)S(1)}, u32[]{:S(2)}, u32[]{:S(2)}) async-start(bf16[16,14,1024]{2,1,0:T(8,128)(2,1)} %copy.348), calls=%async_computation.7 | async-start | bytes 1048576 | tf_op jit(solution)/shard_map/all_to_all | solution.py:116
  247.5 19.6 %all-to-all-start.9 = ((bf16[16,14,1024]{2,1,0:T(8,128)(2,1)}), bf16[16,14,1024]{2,1,0:T(8,128)(2,1)S(1)}, u32[]{:S(2)}, u32[]{:S(2)}) async-start(bf16[16,14,1024]{2,1,0:T(8,128)(2,1)} %get-tuple-element.59), calls=%async_computation.9 | async-start | bytes 1048576 | tf_op jit(solution)/shard_map/all_to_all | solution.py:77
  275.7 17.0 %all-to-all-start.11 = ((bf16[16,14,1024]{2,1,0:T(8,128)(2,1)}), bf16[16,14,1024]{2,1,0:T(8,128)(2,1)S(1)}, u32[]{:S(2)}, u32[]{:S(2)}) async-start(bf16[16,14,1024]{2,1,0:T(8,128)(2,1)} %get-tuple-element.65), calls=%async_computation.11 | async-start | bytes 1048576 | tf_op jit(solution)/shard_map/all_to_all | solution.py:77
  296.9 18.6 %all-to-all-start.13 = ((bf16[16,14,1024]{2,1,0:T(8,128)(2,1)}), bf16[16,14,1024]{2,1,0:T(8,128)(2,1)S(1)}, u32[]{:S(2)}, u32[]{:S(2)}) async-start(bf16[16,14,1024]{2,1,0:T(8,128)(2,1)} %get-tuple-element.71), calls=%async_computation.13 | async-start | bytes 1048576 | tf_op jit(solution)/shard_map/all_to_all | solution.py:77
  300.6 13.2 %collective-permute-start.15 = (bf16[2,8,1,14,768]{4,1,3,2,0:T(8,128)(2,1)S(1)}, bf16[2,8,1,14,768]{4,1,3,2,0:T(8,128)(2,1)S(1)}, u32[]{:S(2)}, u32[]{:S(2)}) collective-permute-start(bf16[2,8,1,14,768]{4,1,3,2,0:T(8,128)(2,1)S(1)} %pad_maximum_fusion.6), channel_id=1, source_target_pairs={{0,8},{8,0},{1,9},{9,1},{2,10},{10,2},{3,11},{11,3},{4,12},{12,4},... | collective-permute-start | bytes 1032200 | tf_op jit(solution)/shard_map/ppermute | solution.py:101
  315.5 21.8 %all-to-all-start.10 = ((bf16[16,14,1024]{2,1,0:T(8,128)(2,1)}), bf16[16,14,1024]{2,1,0:T(8,128)(2,1)S(1)}, u32[]{:S(2)}, u32[]{:S(2)}) async-start(bf16[16,14,1024]{2,1,0:T(8,128)(2,1)} %copy.365), calls=%async_computation.10 | async-start | bytes 1048576 | tf_op jit(solution)/shard_map/all_to_all | solution.py:116
  337.2 18.7 %all-to-all-start.12 = ((bf16[16,14,1024]{2,1,0:T(8,128)(2,1)}), bf16[16,14,1024]{2,1,0:T(8,128)(2,1)S(1)}, u32[]{:S(2)}, u32[]{:S(2)}) async-start(bf16[16,14,1024]{2,1,0:T(8,128)(2,1)} %copy.374), calls=%async_computation.12 | async-start | bytes 1048576 | tf_op jit(solution)/shard_map/all_to_all | solution.py:116
  341.7 17.9 %collective-permute-start.17 = (bf16[2,8,1,14,768]{4,1,3,2,0:T(8,128)(2,1)}, bf16[2,8,1,14,768]{4,1,3,2,0:T(8,128)(2,1)S(1)}, u32[]{:S(2)}, u32[]{:S(2)}) collective-permute-start(bf16[2,8,1,14,768]{4,1,3,2,0:T(8,128)(2,1)} %pad_maximum_fusion.7), channel_id=1, source_target_pairs={{0,8},{8,0},{1,9},{9,1},{2,10},{10,2},{3,11},{11,3},{4,12},{12,4},... | collective-permute-start | bytes 1032200 | tf_op jit(solution)/shard_map/ppermute | solution.py:101
  356.0 19.9 %all-to-all-start.14 = ((bf16[16,14,1024]{2,1,0:T(8,128)(2,1)}), bf16[16,14,1024]{2,1,0:T(8,128)(2,1)S(1)}, u32[]{:S(2)}, u32[]{:S(2)}) async-start(bf16[16,14,1024]{2,1,0:T(8,128)(2,1)} %copy.383), calls=%async_computation.14 | async-start | bytes 1048576 | tf_op jit(solution)/shard_map/all_to_all | solution.py:116
  375.9 14.3 %all-to-all-start.15 = ((bf16[16,14,1024]{2,1,0:T(8,128)(2,1)}), bf16[16,14,1024]{2,1,0:T(8,128)(2,1)S(1)}, u32[]{:S(2)}, u32[]{:S(2)}) async-start(bf16[16,14,1024]{2,1,0:T(8,128)(2,1)} %copy.390), calls=%async_computation.15 | async-start | bytes 1048576 | tf_op jit(solution)/shard_map/all_to_all | solution.py:116
  (37 other events, 645.6 us)
Sparse Core Ops, SparseCore 0:
  9.5 27.4 all-gather.5
  38.6 25.8 all-gather.3
  66.0 25.8 all-gather.7
